TPU v7x, 32 devices: a whole 2x2x4 slice. The times are simulated.
32 devices in a mesh: groups: 2 (over y), pix: 4 (over z), sub: 2 (over x), inner: 2 (over core).
Axes of the slice: x: 2, y: 2, z: 4, core: 2. Of those that a mesh axis runs over, the one named last changes fastest.
Arguments:
- cube: bfloat16 [20480, 256], P(('groups', 'pix', 'sub', 'inner')), parts along dimension 0, may hold values from -70 to 70
Outputs:
- spectra: bfloat16 [256, 16, 1280], P(('pix', 'sub'), 'groups', 'inner'), parts along dimension 1
There are 2 independent parts, one for each index of `groups`. A program takes and returns all parts, laid end to end along the dimension named above; each array names one. Nothing has to cross between parts.
All inputs are finite; a program needn't handle non-finite values.
Results may differ from a plain program's by a relative error of at most 0.0067.
Values may be sent and summed in bfloat16 or wider, within the bound.
No kernel may reach another device: no remote copies, remote signals or barrier semaphores. Data moves between devices by JAX's collectives and lax.ppermute only.
A program may use at most 64 MiB of HBM per device.

v0:
```python
import math

import jax
import jax.numpy as jnp
from jax import lax
from jax.sharding import PartitionSpec as P

MODES = 32
ITERS = 4


def matmul_high(left, right):
    return jnp.dot(left, right, precision=lax.Precision.HIGHEST)


def leading_modes(gram_matrix, width_count, sweeps):
    mode_basis = jnp.eye(gram_matrix.shape[0], width_count, dtype=jnp.float32)
    for iteration in range(sweeps):
        product = matmul_high(gram_matrix, mode_basis)
        cross_gram = matmul_high(product.T, product)
        lower_factor = jnp.linalg.cholesky(cross_gram)
        mode_basis = jax.scipy.linalg.solve_triangular(lower_factor, product.T, lower=True).T
    return mode_basis


def delay_table(channels):
    middle = channels // 2
    row_index = lax.broadcasted_iota(jnp.int32, (channels, channels), 0)
    col_index = lax.broadcasted_iota(jnp.int32, (channels, channels), 1)
    harmonic = jnp.where(row_index <= middle, row_index, row_index - middle)
    angles = (harmonic * col_index % channels).astype(jnp.float32) * (2.0 * math.pi / channels)
    values = jnp.where(row_index <= middle, jnp.cos(angles), jnp.sin(angles)) / math.sqrt(channels)
    return values.astype(jnp.bfloat16)


def local(cube):
    pixels, channels = cube.shape
    pixel_count = pixels * lax.axis_size(("pix", "sub", "inner"))
    partial_gram = lax.dot_general(
        cube, cube, (((0,), (0,)), ((), ())), preferred_element_type=jnp.float32
    )
    gram_matrix = lax.psum(partial_gram, ("pix", "sub", "inner"))
    gram_matrix = gram_matrix / pixel_count
    mode_basis = leading_modes(gram_matrix, MODES, ITERS)
    modes_b = mode_basis.astype(jnp.bfloat16)
    amplitudes = jnp.dot(cube, modes_b, preferred_element_type=jnp.float32).astype(jnp.bfloat16)
    cleaned = (cube - jnp.dot(amplitudes, modes_b.T, preferred_element_type=jnp.float32)).astype(
        jnp.bfloat16
    )
    table_b = delay_table(channels)
    coefficients = lax.dot_general(
        table_b, cleaned, (((1,), (1,)), ((), ())), preferred_element_type=jnp.float32
    ).astype(jnp.bfloat16)
    spectra = lax.all_to_all(
        coefficients[:, None, :], ("pix", "sub"), split_axis=0, concat_axis=1, tiled=True
    )
    return spectra


def solution(mesh):
    return jax.shard_map(
        local,
        mesh=mesh,
        in_specs=(P(("groups", "pix", "sub", "inner"), None),),
        out_specs=P(("pix", "sub"), "groups", "inner"),
        check_vma=False,
    )
```

profile of v0, /device:TPU:0, one launch (start us, length us, event | category | flops | bytes accessed | tf_op | source)
XLA Modules:
  0.0 160.6 jit_solution(15145366954899768476)
XLA Ops:
  6.5 0.0 all-reduce.2.cloned.1.call-start
  6.5 2.1 %fusion.59 = f32[256,256]{1,0:T(8,128)} fusion(bf16[640,256]{1,0:T(8,128)(2,1)} %param.4), kind=kOutput, calls=%fused_computation.85 | convolution fusion | flops 83886080 | bytes 589824 | tf_op jit(solution)/shard_map/dot_general | solution.py:39
  8.6 0.0 all-reduce.2.cloned.1.call-update
  8.7 94.6 %all-reduce.2.cloned.1.call-done = f32[256,256]{1,0:T(8,128)} async-done(((f32[256,256]{1,0:T(8,128)}), f32[256,256]{1,0:T(8,128)}) %all-reduce.2.cloned.1.call-update) | async-done | bytes 262160 | tf_op jit(solution)/shard_map/psum | solution.py:42
  103.3 0.0 copy-start
  103.3 1.3 fusion.12
  104.6 0.2 fusion.60
  104.7 0.1 copy.13
  104.8 2.9 %cholesky.74 = f32[32,32]{1,0:T(8,128)S(1)} custom-call(f32[32,32]{1,0:T(8,128)S(1)} %fusion.43), custom_call_target="Cholesky" | custom-call | tf_op jit(solution)/shard_map/jit(cholesky)/cholesky | solution.py:21
  107.8 0.6 compare_reduce_fusion.3
  108.4 0.7 fusion.32
  109.1 2.4 %custom-call.8 = f32[1,32,32]{1,2,0:T(8,128)S(1)} custom-call(f32[1,32,32]{2,1,0:T(8,128)S(1)} %fusion.32), custom_call_target="InvertDiagBlocksLowerTriangular" | custom-call | tf_op jit(solution)/shard_map/jit(_solve_triangular)/triangular_solve | solution.py:22
  111.5 0.2 fusion.30
  111.8 0.0 copy-done
  111.8 0.3 fusion.10
  112.1 0.2 fusion.61
  112.3 0.1 copy.14
  112.4 2.9 %cholesky.85 = f32[32,32]{1,0:T(8,128)S(1)} custom-call(f32[32,32]{1,0:T(8,128)S(1)} %fusion.41), custom_call_target="Cholesky" | custom-call | tf_op jit(solution)/shard_map/jit(cholesky)/cholesky | solution.py:21
  115.3 0.6 compare_reduce_fusion.2
  116.0 0.7 fusion.33
  116.6 2.4 %custom-call.9 = f32[1,32,32]{1,2,0:T(8,128)S(1)} custom-call(f32[1,32,32]{2,1,0:T(8,128)S(1)} %fusion.33), custom_call_target="InvertDiagBlocksLowerTriangular" | custom-call | tf_op jit(solution)/shard_map/jit(_solve_triangular)/triangular_solve | solution.py:22
  119.1 0.2 fusion.28
  119.3 0.3 fusion.8
  119.7 0.2 fusion.62
  119.8 0.1 copy.15
  119.9 2.9 %cholesky.96 = f32[32,32]{1,0:T(8,128)S(1)} custom-call(f32[32,32]{1,0:T(8,128)S(1)} %fusion.39), custom_call_target="Cholesky" | custom-call | tf_op jit(solution)/shard_map/jit(cholesky)/cholesky | solution.py:21
  122.9 0.6 compare_reduce_fusion.1
  123.5 0.7 fusion.34
  124.2 2.4 %custom-call.10 = f32[1,32,32]{1,2,0:T(8,128)S(1)} custom-call(f32[1,32,32]{2,1,0:T(8,128)S(1)} %fusion.34), custom_call_target="InvertDiagBlocksLowerTriangular" | custom-call | tf_op jit(solution)/shard_map/jit(_solve_triangular)/triangular_solve | solution.py:22
  126.6 0.0 copy-start.1
  126.6 0.2 fusion.26
  126.9 0.3 fusion.6
  127.2 0.2 fusion.63
  127.4 0.1 copy.16
  127.5 2.9 %cholesky.107 = f32[32,32]{1,0:T(8,128)S(1)} custom-call(f32[32,32]{1,0:T(8,128)S(1)} %fusion.37), custom_call_target="Cholesky" | custom-call | tf_op jit(solution)/shard_map/jit(cholesky)/cholesky | solution.py:21
  130.4 0.6 compare_reduce_fusion
  131.1 0.7 fusion.35
  131.7 2.4 %custom-call.11 = f32[1,32,32]{1,2,0:T(8,128)S(1)} custom-call(f32[1,32,32]{2,1,0:T(8,128)S(1)} %fusion.35), custom_call_target="InvertDiagBlocksLowerTriangular" | custom-call | tf_op jit(solution)/shard_map/jit(_solve_triangular)/triangular_solve | solution.py:22
  134.2 0.2 convolution_convert_fusion.2
  134.4 0.0 copy-done.1
  134.4 0.2 convolution_convert_fusion.1
  134.6 1.5 fusion.1
  136.1 0.5 broadcast.63
  136.6 0.8 reduce.4
  137.5 0.1 reshape.8
  137.6 15.0 %all_to_all.18 = bf16[8,2,10240]{2,1,0:T(2,128)(2,1)S(1)} all-to-all(bf16[8,2,10240]{2,1,0:T(2,128)(2,1)S(1)} %reshape.8), channel_id=1, replica_groups=mesh['groups'=2,'pix'=4,'sub'=2,'inner'=2] {'pix','sub'}, dimensions={0} | all-to-all | bytes 655360 | tf_op jit(solution)/shard_map/all_to_all | solution.py:54
  152.5 0.3 reshape.9
  152.9 0.8 copy.18
  (11 shorter events, 0.2 us)
Async XLA Ops:
  6.5 96.7 %all-reduce.2.cloned.1.call-start = ((), (), s32[]{:S(2)}) async-start(), calls=%async_computation.1 | async-start | bytes 524288 | tf_op jit(solution)/shard_map/psum | solution.py:42
  103.3 8.5 %copy-start = (f32[256,256]{1,0:T(8,128)S(1)}, f32[256,256]{1,0:T(8,128)}, u32[]{:S(2)}) copy-start(f32[256,256]{1,0:T(8,128)} %all-reduce.2.cloned.1.call-done) | copy-start | bytes 786436
  126.6 7.8 %copy-start.1 = (bf16[640,256]{1,0:T(8,128)(2,1)S(1)}, bf16[640,256]{1,0:T(8,128)(2,1)}, u32[]{:S(2)}) copy-start(bf16[640,256]{1,0:T(8,128)(2,1)} %param.4) | copy-start | bytes 983044
Sparse Core Ops, SparseCore 0:
  10.7 92.4 all-reduce.1
where the time goes:
time: 161 us
  waiting for transfers between devices  94.6 us (59%)
  other arithmetic  27.6 us (17%)
  blocking collectives  15 us (9%)
  between operations  13.6 us (8%)
  matrix products  7.73 us (5%)
  local copies, waits for them, and re-layouts  2.08 us (1%)
    psum x1, waiting for transfers between devices, local(): gram_matrix = lax.psum(partial_gram, ('pix', 'sub', 'inner'))  94.6 us
    all_to_all x1, blocking collectives, local(): lax.all_to_all(coefficients[:, None, :], ('pix', 'sub'), split_axis=0, co...  15 us
    another operation x12, other arithmetic, leading_modes(): lower_factor = jnp.linalg.cholesky(cross_gram)  14.4 us
    another operation x8, other arithmetic, leading_modes(): jax.scipy.linalg.solve_triangular(lower_factor, product.T, lower=True)  12.3 us
  transfers between devices with their start and end apart: 1, of which 1 were waited for; matrix products, arithmetic and copies ran while one was open for 0% of the time, Pallas kernels for 0%

commit v1 on v0

v1 whole, which is shorter than its diff:
```python
import math

import jax
import jax.numpy as jnp
from jax import lax
from jax.sharding import PartitionSpec as P

MODES = 32
ITERS = 4
VARIANT = "symbutterfly"


def matmul_high(left, right):
    return jnp.dot(left, right, precision=lax.Precision.HIGHEST)


def leading_modes(gram_matrix, width_count, sweeps):
    mode_basis = jnp.eye(gram_matrix.shape[0], width_count, dtype=jnp.float32)
    for iteration in range(sweeps):
        product = matmul_high(gram_matrix, mode_basis)
        cross_gram = matmul_high(product.T, product)
        lower_factor = jnp.linalg.cholesky(cross_gram)
        mode_basis = jax.scipy.linalg.solve_triangular(lower_factor, product.T, lower=True).T
    return mode_basis


def delay_table(channels):
    middle = channels // 2
    row_index = lax.broadcasted_iota(jnp.int32, (channels, channels), 0)
    col_index = lax.broadcasted_iota(jnp.int32, (channels, channels), 1)
    harmonic = jnp.where(row_index <= middle, row_index, row_index - middle)
    angles = (harmonic * col_index % channels).astype(jnp.float32) * (2.0 * math.pi / channels)
    values = jnp.where(row_index <= middle, jnp.cos(angles), jnp.sin(angles)) / math.sqrt(channels)
    return values.astype(jnp.bfloat16)


def steps_of(sizes):
    out = []
    for name, n in sizes:
        d = 1
        while d < n:
            out.append((name, n, d))
            d *= 2
    return out


def butterfly_sum(x, sizes):
    for name, n, d in steps_of(sizes):
        x = x + lax.ppermute(x, name, [(i, i ^ d) for i in range(n)])
    return x


def halving_sum(x, sizes):
    steps = steps_of(sizes)
    for name, n, d in steps:
        bit = (lax.axis_index(name) // d) % 2
        half = x.shape[0] // 2
        lo, hi = x[:half], x[half:]
        send = jnp.where(bit == 0, hi, lo)
        keep = jnp.where(bit == 0, lo, hi)
        x = keep + lax.ppermute(send, name, [(i, i ^ d) for i in range(n)])
    for name, n, d in reversed(steps):
        bit = (lax.axis_index(name) // d) % 2
        other = lax.ppermute(x, name, [(i, i ^ d) for i in range(n)])
        x = jnp.where(bit == 0, jnp.concatenate([x, other]), jnp.concatenate([other, x]))
    return x


def make_local(sizes):
    def reduce(g):
        if VARIANT == "psum":
            return lax.psum(g, ("pix", "sub", "inner"))
        if VARIANT == "butterfly":
            return butterfly_sum(g, sizes)
        if VARIANT == "halving":
            return halving_sum(g, sizes)
        if VARIANT == "symbutterfly":
            h = g.shape[0] // 2
            packed = jnp.concatenate([g[:h, :h], g[:h, h:], g[h:, h:]], axis=0)
            packed = butterfly_sum(packed, sizes)
            a, b, d = packed[:h], packed[h:2 * h], packed[2 * h:]
            return jnp.concatenate([jnp.concatenate([a, b], 1), jnp.concatenate([b.T, d], 1)], 0)
        raise ValueError(VARIANT)

    def local(cube):
        pixels, channels = cube.shape
        pixel_count = pixels * lax.axis_size(("pix", "sub", "inner"))
        partial_gram = lax.dot_general(
            cube, cube, (((0,), (0,)), ((), ())), preferred_element_type=jnp.float32
        )
        gram_matrix = reduce(partial_gram)
        gram_matrix = gram_matrix / pixel_count
        mode_basis = leading_modes(gram_matrix, MODES, ITERS)
        modes_b = mode_basis.astype(jnp.bfloat16)
        amplitudes = jnp.dot(cube, modes_b, preferred_element_type=jnp.float32).astype(jnp.bfloat16)
        cleaned = (cube - jnp.dot(amplitudes, modes_b.T, preferred_element_type=jnp.float32)).astype(
            jnp.bfloat16
        )
        table_b = delay_table(channels)
        coefficients = lax.dot_general(
            table_b, cleaned, (((1,), (1,)), ((), ())), preferred_element_type=jnp.float32
        ).astype(jnp.bfloat16)
        spectra = lax.all_to_all(
            coefficients[:, None, :], ("pix", "sub"), split_axis=0, concat_axis=1, tiled=True
        )
        return spectra
    return local


def solution(mesh):
    sizes = [(a, mesh.shape[a]) for a in ("inner", "sub", "pix")]
    return jax.shard_map(
        make_local(sizes),
        mesh=mesh,
        in_specs=(P(("groups", "pix", "sub", "inner"), None),),
        out_specs=P(("pix", "sub"), "groups", "inner"),
        check_vma=False,
    )
```

time: 161 us -> 79.2 us (0.49)
  waiting for transfers between devices: 94.6 us -> 18.9 us
  between operations: 13.6 us -> 0.26 us
  starting transfers between devices: 0.01 us -> 7.98 us
  matrix products: 7.73 us -> 6.01 us
    psum x1 -> x0, waiting for transfers between devices: 94.6 us -> none  [local(): gram_matrix = lax.psum(partial_gram, ('pix', 'sub', 'inner'))]
    ppermute x0 -> x4, waiting for transfers between devices: none -> 18.9 us  [butterfly_sum(): x = x + lax.ppermute(x, name, [(i, i ^ d) for i in range(n)])]
    ppermute x0 -> x4, starting transfers between devices: none -> 7.98 us  [butterfly_sum(): x = x + lax.ppermute(x, name, [(i, i ^ d) for i in range(n)])]
  transfers between devices with their start and end apart: 1 -> 4, of which waited for: 1 -> 4; matrix products, arithmetic and copies ran while one was open for 0% -> 0% of each run, Pallas kernels for 0% -> 0%
where the time goes in v1:
time: 79.2 us; the launch traced here: 79 us
  other arithmetic  27.7 us (35%)
  waiting for transfers between devices  18.9 us (24%)
  blocking collectives  16 us (20%)
  starting transfers between devices  7.98 us (10%)
  matrix products  6.01 us (8%)
  local copies, waits for them, and re-layouts  2.2 us (3%)
    ppermute x4, waiting for transfers between devices, butterfly_sum(): x = x + lax.ppermute(x, name, [(i, i ^ d) for i in range(n)])  18.9 us
    all_to_all x1, blocking collectives, local(): lax.all_to_all(coefficients[:, None, :], ('pix', 'sub'), split_axis=0, co...  16 us
    another operation x12, other arithmetic, leading_modes(): lower_factor = jnp.linalg.cholesky(cross_gram)  14.4 us
    another operation x8, other arithmetic, leading_modes(): jax.scipy.linalg.solve_triangular(lower_factor, product.T, lower=True)  12.3 us
    ppermute x4, starting transfers between devices, butterfly_sum(): x = x + lax.ppermute(x, name, [(i, i ^ d) for i in range(n)])  7.98 us
    dot_general x8, matrix products, matmul_high(): return jnp.dot(left, right, precision=lax.Precision.HIGHEST)  1.94 us
  transfers between devices with their start and end apart: 4, of which 4 were waited for; matrix products, arithmetic and copies ran while one was open for 0% of the time, Pallas kernels for 0%

profile of v1, /device:TPU:0, one launch (start us, length us, event | category | flops | bytes accessed | tf_op | source)
XLA Modules:
  0.0 79.0 jit_solution(11939756387512066337)
XLA Ops:
  0.0 1.4 %fusion.49 = f32[256,256]{1,0:T(8,128)S(1)} fusion(bf16[640,256]{1,0:T(8,128)(2,1)} %param.4), kind=kOutput, calls=%fused_computation.78 | convolution fusion | flops 83886080 | bytes 589824 | tf_op jit(solution)/shard_map/dot_general | solution.py:88
  1.4 0.6 collective-permute-start
  2.0 1.1 %collective-permute-done = f32[384,128]{1,0:T(8,128)S(1)} collective-permute-done((f32[384,128]{1,0:T(8,128)S(1)}, f32[384,128]{1,0:T(8,128)S(1)}, u32[]{:S(2)}, u32[]{:S(2)}) %collective-permute-start) | collective-permute-done | bytes 196640 | tf_op jit(solution)/shard_map/ppermute | solution.py:49
  3.1 2.9 %collective-permute-start.1 = (f32[384,128]{1,0:T(8,128)S(1)}, f32[384,128]{1,0:T(8,128)S(1)}, u32[]{:S(2)}, u32[]{:S(2)}) collective-permute-start(f32[384,128]{1,0:T(8,128)S(1)} %fusion.44), channel_id=1, source_target_pairs={{0,2},{2,0},{1,3},{3,1},{4,6},{6,4},{5,7},{7,5},{8,10},{10,8},{9,1... | collective-permute-start | bytes 589832 | tf_op jit(solution)/shard_map/ppermute | solution.py:49
  6.0 5.2 %collective-permute-done.1 = f32[384,128]{1,0:T(8,128)S(1)} collective-permute-done((f32[384,128]{1,0:T(8,128)S(1)}, f32[384,128]{1,0:T(8,128)S(1)}, u32[]{:S(2)}, u32[]{:S(2)}) %collective-permute-start.1) | collective-permute-done | bytes 196640 | tf_op jit(solution)/shard_map/ppermute | solution.py:49
  11.2 1.9 %collective-permute-start.2 = (f32[384,128]{1,0:T(8,128)S(1)}, f32[384,128]{1,0:T(8,128)S(1)}, u32[]{:S(2)}, u32[]{:S(2)}) collective-permute-start(f32[384,128]{1,0:T(8,128)S(1)} %add.30), channel_id=1, source_target_pairs={{0,4},{4,0},{8,12},{12,8},{1,5},{5,1},{9,13},{13,9},{2,6},{6,2},{1... | collective-permute-start | bytes 589832 | tf_op jit(solution)/shard_map/ppermute | solution.py:49
  13.1 4.5 %collective-permute-done.2 = f32[384,128]{1,0:T(8,128)S(1)} collective-permute-done((f32[384,128]{1,0:T(8,128)S(1)}, f32[384,128]{1,0:T(8,128)S(1)}, u32[]{:S(2)}, u32[]{:S(2)}) %collective-permute-start.2) | collective-permute-done | bytes 196640 | tf_op jit(solution)/shard_map/ppermute | solution.py:49
  17.7 2.6 %collective-permute-start.3 = (f32[384,128]{1,0:T(8,128)S(1)}, f32[384,128]{1,0:T(8,128)S(1)}, u32[]{:S(2)}, u32[]{:S(2)}) collective-permute-start(f32[384,128]{1,0:T(8,128)S(1)} %add.31), channel_id=1, source_target_pairs={{0,8},{4,12},{8,0},{12,4},{1,9},{5,13},{9,1},{13,5},{2,10},{6,14},... | collective-permute-start | bytes 589832 | tf_op jit(solution)/shard_map/ppermute | solution.py:49
  20.3 8.1 %collective-permute-done.3 = f32[384,128]{1,0:T(8,128)S(1)} collective-permute-done((f32[384,128]{1,0:T(8,128)S(1)}, f32[384,128]{1,0:T(8,128)S(1)}, u32[]{:S(2)}, u32[]{:S(2)}) %collective-permute-start.3) | collective-permute-done | bytes 196640 | tf_op jit(solution)/shard_map/ppermute | solution.py:49
  28.4 0.1 copy.15
  28.5 0.3 fusion.13
  28.8 0.2 fusion.50
  29.0 0.1 copy.16
  29.1 2.9 %cholesky.74 = f32[32,32]{1,0:T(8,128)S(1)} custom-call(f32[32,32]{1,0:T(8,128)S(1)} %fusion.32), custom_call_target="Cholesky" | custom-call | tf_op jit(solution)/shard_map/jit(cholesky)/cholesky | solution.py:22
  32.0 0.6 compare_reduce_fusion.3
  32.7 0.7 fusion.21
  33.3 2.4 %custom-call.8 = f32[1,32,32]{1,2,0:T(8,128)S(1)} custom-call(f32[1,32,32]{2,1,0:T(8,128)S(1)} %fusion.21), custom_call_target="InvertDiagBlocksLowerTriangular" | custom-call | tf_op jit(solution)/shard_map/jit(_solve_triangular)/triangular_solve | solution.py:23
  35.7 0.2 fusion.19
  36.0 0.3 fusion.47
  36.4 0.2 fusion.51
  36.5 0.1 copy.17
  36.6 2.9 %cholesky.85 = f32[32,32]{1,0:T(8,128)S(1)} custom-call(f32[32,32]{1,0:T(8,128)S(1)} %fusion.30), custom_call_target="Cholesky" | custom-call | tf_op jit(solution)/shard_map/jit(cholesky)/cholesky | solution.py:22
  39.6 0.6 compare_reduce_fusion.2
  40.2 0.7 fusion.22
  40.9 2.4 %custom-call.9 = f32[1,32,32]{1,2,0:T(8,128)S(1)} custom-call(f32[1,32,32]{2,1,0:T(8,128)S(1)} %fusion.22), custom_call_target="InvertDiagBlocksLowerTriangular" | custom-call | tf_op jit(solution)/shard_map/jit(_solve_triangular)/triangular_solve | solution.py:23
  43.3 0.2 fusion.17
  43.5 0.3 fusion.46
  43.9 0.2 fusion.52
  44.1 0.1 copy.18
  44.1 2.9 %cholesky.96 = f32[32,32]{1,0:T(8,128)S(1)} custom-call(f32[32,32]{1,0:T(8,128)S(1)} %fusion.28), custom_call_target="Cholesky" | custom-call | tf_op jit(solution)/shard_map/jit(cholesky)/cholesky | solution.py:22
  47.1 0.6 compare_reduce_fusion.1
  47.7 0.7 fusion.23
  48.4 2.4 %custom-call.10 = f32[1,32,32]{1,2,0:T(8,128)S(1)} custom-call(f32[1,32,32]{2,1,0:T(8,128)S(1)} %fusion.23), custom_call_target="InvertDiagBlocksLowerTriangular" | custom-call | tf_op jit(solution)/shard_map/jit(_solve_triangular)/triangular_solve | solution.py:23
  50.8 0.2 fusion.15
  51.1 0.0 copy-start
  51.1 0.3 fusion.45
  51.5 0.2 fusion.53
  51.6 0.1 copy.19
  51.7 2.9 %cholesky.107 = f32[32,32]{1,0:T(8,128)S(1)} custom-call(f32[32,32]{1,0:T(8,128)S(1)} %fusion.26), custom_call_target="Cholesky" | custom-call | tf_op jit(solution)/shard_map/jit(cholesky)/cholesky | solution.py:22
  54.7 0.6 compare_reduce_fusion
  55.3 0.7 fusion.24
  56.0 2.4 %custom-call.11 = f32[1,32,32]{1,2,0:T(8,128)S(1)} custom-call(f32[1,32,32]{2,1,0:T(8,128)S(1)} %fusion.24), custom_call_target="InvertDiagBlocksLowerTriangular" | custom-call | tf_op jit(solution)/shard_map/jit(_solve_triangular)/triangular_solve | solution.py:23
  58.4 0.2 convolution_convert_fusion.2
  58.6 0.0 copy-done
  58.7 0.2 convolution_convert_fusion.1
  58.9 1.5 %fusion.1 = bf16[256,1,640]{2,0,1:T(8,128)(2,1)S(1)} fusion(bf16[32,640]{1,0:T(8,128)(2,1)S(1)} %convolution_convert_fusion.1, bf16[32,256]{1,0:T(8,128)(2,1)S(1)} %convolution_convert_fusion.2, bf16[640,256]{1,0:T(8,128)(2,1)S(1)} %copy-done, s32[256]{0:T(256)S(1)} %iota_add_fusion, pred[256]{0:T(512)(128)(4,1)S(1)} %iota_compare_fusion.4), kind=kOutput, calls=%fused_computation.3 | convolution fusion | flops 96206848 | bytes 713984 | tf_op jit(solution)/shard_map/dot_general | solution.py:100
  60.4 0.5 broadcast.63
  60.9 0.8 %reduce.4 = bf16[256,640]{1,0:T(8,128)(2,1)S(1)} reduce(bf16[256,1,640]{2,0,1:T(8,128)(2,1)S(1)} %fusion.1, bf16[]{:T(256)} %broadcast.63), dimensions={1}, to_apply=%copy.20.reduce_sub_computation | reduce | bytes 655362 | tf_op jit(solution)/shard_map/broadcast_in_dim | solution.py:104
  61.7 0.1 reshape.8
  61.8 16.0 %all_to_all.18 = bf16[8,2,10240]{2,1,0:T(2,128)(2,1)S(1)} all-to-all(bf16[8,2,10240]{2,1,0:T(2,128)(2,1)S(1)} %reshape.8), channel_id=1, replica_groups=mesh['groups'=2,'pix'=4,'sub'=2,'inner'=2] {'pix','sub'}, dimensions={0} | all-to-all | bytes 655360 | tf_op jit(solution)/shard_map/all_to_all | solution.py:103
  77.8 0.3 reshape.9
  78.2 0.8 %copy.21 = bf16[32,8,640]{2,1,0:T(8,128)(2,1)} copy(bf16[32,8,640]{2,0,1:T(8,128)(2,1)S(1)} %bitcast.74) | data formatting | bytes 655360 | tf_op jit(solution)/shard_map/all_to_all | solution.py:103
  (19 shorter events, 0.3 us)
Async XLA Ops:
  1.4 1.6 %collective-permute-start = (f32[384,128]{1,0:T(8,128)S(1)}, f32[384,128]{1,0:T(8,128)S(1)}, u32[]{:S(2)}, u32[]{:S(2)}) collective-permute-start(f32[384,128]{1,0:T(8,128)S(1)} %pad_maximum_fusion), channel_id=1, source_target_pairs={{0,1},{1,0},{2,3},{3,2},{4,5},{5,4},{6,7},{7,6},{8,9},{9,8},{10,11... | collective-permute-start | bytes 589832 | tf_op jit(solution)/shard_map/ppermute | solution.py:49
  3.1 8.1 %collective-permute-start.1 = (f32[384,128]{1,0:T(8,128)S(1)}, f32[384,128]{1,0:T(8,128)S(1)}, u32[]{:S(2)}, u32[]{:S(2)}) collective-permute-start(f32[384,128]{1,0:T(8,128)S(1)} %fusion.44), channel_id=1, source_target_pairs={{0,2},{2,0},{1,3},{3,1},{4,6},{6,4},{5,7},{7,5},{8,10},{10,8},{9,1... | collective-permute-start | bytes 589832 | tf_op jit(solution)/shard_map/ppermute | solution.py:49
  11.2 6.4 %collective-permute-start.2 = (f32[384,128]{1,0:T(8,128)S(1)}, f32[384,128]{1,0:T(8,128)S(1)}, u32[]{:S(2)}, u32[]{:S(2)}) collective-permute-start(f32[384,128]{1,0:T(8,128)S(1)} %add.30), channel_id=1, source_target_pairs={{0,4},{4,0},{8,12},{12,8},{1,5},{5,1},{9,13},{13,9},{2,6},{6,2},{1... | collective-permute-start | bytes 589832 | tf_op jit(solution)/shard_map/ppermute | solution.py:49
  17.7 10.7 %collective-permute-start.3 = (f32[384,128]{1,0:T(8,128)S(1)}, f32[384,128]{1,0:T(8,128)S(1)}, u32[]{:S(2)}, u32[]{:S(2)}) collective-permute-start(f32[384,128]{1,0:T(8,128)S(1)} %add.31), channel_id=1, source_target_pairs={{0,8},{4,12},{8,0},{12,4},{1,9},{5,13},{9,1},{13,5},{2,10},{6,14},... | collective-permute-start | bytes 589832 | tf_op jit(solution)/shard_map/ppermute | solution.py:49
  51.1 7.6 %copy-start = (bf16[640,256]{1,0:T(8,128)(2,1)S(1)}, bf16[640,256]{1,0:T(8,128)(2,1)}, u32[]{:S(2)}) copy-start(bf16[640,256]{1,0:T(8,128)(2,1)} %param.4) | copy-start | bytes 983044

commit v2 on v1

--- a/solution.py
+++ b/solution.py
@@ -3,11 +3,45 @@
 import jax
 import jax.numpy as jnp
 from jax import lax
+from jax.experimental import pallas as pl
+from jax.experimental.pallas import tpu as pltpu
 from jax.sharding import PartitionSpec as P
 
 MODES = 32
 ITERS = 4
 VARIANT = "symbutterfly"
+HI = lax.Precision.HIGHEST
+
+
+def modes_kernel(g_ref, out_ref):
+    g = g_ref[...]
+    m = out_ref.shape[0]
+    rows = lax.broadcasted_iota(jnp.int32, (m, 1), 0)
+    cols = lax.broadcasted_iota(jnp.int32, (1, m), 1)
+    xt = g[:m, :]
+    for it in range(ITERS):
+        pt = xt if it == 0 else jnp.dot(xt, g, precision=HI, preferred_element_type=jnp.float32)
+        c = lax.dot_general(pt, pt, (((1,), (1,)), ((), ())), precision=HI,
+                            preferred_element_type=jnp.float32)
+        xt = pt
+        for j in range(m):
+            d = jnp.sqrt(c[j:j + 1, j:j + 1])
+            q = xt[j:j + 1, :] / d
+            rcol = jnp.where(rows > j, c[:, j:j + 1] / d, 0.0)
+            rrow = jnp.where(cols > j, c[j:j + 1, :] / d, 0.0)
+            xt = jnp.where(rows == j, q, xt - rcol * q)
+            c = c - rcol * rrow
+    out_ref[...] = xt
+
+
+def leading_modes_t(gram):
+    n = gram.shape[0]
+    return pl.pallas_call(
+        modes_kernel,
+        out_shape=jax.ShapeDtypeStruct((MODES, n), jnp.float32),
+        in_specs=[pl.BlockSpec(memory_space=pltpu.VMEM)],
+        out_specs=pl.BlockSpec(memory_space=pltpu.VMEM),
+    )(gram)
 
 
 def matmul_high(left, right):
@@ -90,8 +124,7 @@
         )
         gram_matrix = reduce(partial_gram)
         gram_matrix = gram_matrix / pixel_count
-        mode_basis = leading_modes(gram_matrix, MODES, ITERS)
-        modes_b = mode_basis.astype(jnp.bfloat16)
+        modes_b = leading_modes_t(gram_matrix).T.astype(jnp.bfloat16)
         amplitudes = jnp.dot(cube, modes_b, preferred_element_type=jnp.float32).astype(jnp.bfloat16)
         cleaned = (cube - jnp.dot(amplitudes, modes_b.T, preferred_element_type=jnp.float32)).astype(
             jnp.bfloat16

time: 79.2 us -> 65.7 us (0.83)
  other arithmetic: 27.7 us -> 1.66 us
  Pallas kernels: 0 us -> 15 us
  matrix products: 6.01 us -> 3.91 us
    another operation x20 -> x0, other arithmetic: 26.7 us -> none  [the longest x12 14.4 us: leading_modes(): lower_factor = jnp.linalg.cholesky(cross_gram)]
    pallas_call x0 -> x1, Pallas kernels: none -> 15 us  [leading_modes_t(): pl.pallas_call(modes_kernel, out_shape=jax.ShapeDtypeStruct((MODES, n), j...]
    dot_general x8 -> x0, matrix products: 1.94 us -> none  [matmul_high(): return jnp.dot(left, right, precision=lax.Precision.HIGHEST)]
    another operation x4 -> x0, matrix products: 0.98 us -> none  [leading_modes(): jax.scipy.linalg.solve_triangular(lower_factor, product.T, lower=True)]
    dot_general x1, matrix products: 0.2 us -> 1.03 us  [local(): jnp.dot(cube, modes_b, preferred_element_type=jnp.float32)]
where the time goes in v2:
time: 65.7 us; the launch traced here: 65.5 us
  waiting for transfers between devices  18.9 us (29%)
  blocking collectives  16 us (24%)
  Pallas kernels  15 us (23%)
  starting transfers between devices  7.98 us (12%)
  matrix products  3.91 us (6%)
  local copies, waits for them, and re-layouts  1.92 us (3%)
  other arithmetic  1.66 us (3%)
    ppermute x4, waiting for transfers between devices, butterfly_sum(): x = x + lax.ppermute(x, name, [(i, i ^ d) for i in range(n)])  18.9 us
    all_to_all x1, blocking collectives, local(): lax.all_to_all(coefficients[:, None, :], ('pix', 'sub'), split_axis=0, co...  16 us
    pallas_call x1, Pallas kernels, leading_modes_t(): pl.pallas_call(modes_kernel, out_shape=jax.ShapeDtypeStruct((MODES, n), j...  15 us
    ppermute x4, starting transfers between devices, butterfly_sum(): x = x + lax.ppermute(x, name, [(i, i ^ d) for i in range(n)])  7.98 us
    dot_general x1, matrix products, local(): lax.dot_general(table_b, cleaned, (((1,), (1,)), ((), ())), preferred_ele...  1.51 us
    dot_general x1, matrix products, local(): lax.dot_general(cube, cube, (((0,), (0,)), ((), ())), preferred_element_t...  1.37 us
  transfers between devices with their start and end apart: 4, of which 4 were waited for; matrix products, arithmetic and copies ran while one was open for 0% of the time, Pallas kernels for 0%

profile of v2, /device:TPU:0, one launch (start us, length us, event | category | flops | bytes accessed | tf_op | source)
XLA Modules:
  0.0 65.5 jit_solution(2746977444669607255)
XLA Ops:
  0.0 1.4 %fusion.23 = f32[256,256]{1,0:T(8,128)S(1)} fusion(bf16[640,256]{1,0:T(8,128)(2,1)} %param.1), kind=kOutput, calls=%fused_computation.34 | convolution fusion | flops 83886080 | bytes 589824 | tf_op jit(solution)/shard_map/dot_general | solution.py:122
  1.4 0.6 collective-permute-start
  2.0 1.1 %collective-permute-done = f32[384,128]{1,0:T(8,128)S(1)} collective-permute-done((f32[384,128]{1,0:T(8,128)S(1)}, f32[384,128]{1,0:T(8,128)S(1)}, u32[]{:S(2)}, u32[]{:S(2)}) %collective-permute-start) | collective-permute-done | bytes 196640 | tf_op jit(solution)/shard_map/ppermute | solution.py:83
  3.1 2.9 %collective-permute-start.1 = (f32[384,128]{1,0:T(8,128)S(1)}, f32[384,128]{1,0:T(8,128)S(1)}, u32[]{:S(2)}, u32[]{:S(2)}) collective-permute-start(f32[384,128]{1,0:T(8,128)S(1)} %fusion.21), channel_id=1, source_target_pairs={{0,2},{2,0},{1,3},{3,1},{4,6},{6,4},{5,7},{7,5},{8,10},{10,8},{9,1... | collective-permute-start | bytes 589832 | tf_op jit(solution)/shard_map/ppermute | solution.py:83
  6.0 5.2 %collective-permute-done.1 = f32[384,128]{1,0:T(8,128)S(1)} collective-permute-done((f32[384,128]{1,0:T(8,128)S(1)}, f32[384,128]{1,0:T(8,128)S(1)}, u32[]{:S(2)}, u32[]{:S(2)}) %collective-permute-start.1) | collective-permute-done | bytes 196640 | tf_op jit(solution)/shard_map/ppermute | solution.py:83
  11.2 1.9 %collective-permute-start.2 = (f32[384,128]{1,0:T(8,128)S(1)}, f32[384,128]{1,0:T(8,128)S(1)}, u32[]{:S(2)}, u32[]{:S(2)}) collective-permute-start(f32[384,128]{1,0:T(8,128)S(1)} %add.21), channel_id=1, source_target_pairs={{0,4},{4,0},{8,12},{12,8},{1,5},{5,1},{9,13},{13,9},{2,6},{6,2},{1... | collective-permute-start | bytes 589832 | tf_op jit(solution)/shard_map/ppermute | solution.py:83
  13.1 4.5 %collective-permute-done.2 = f32[384,128]{1,0:T(8,128)S(1)} collective-permute-done((f32[384,128]{1,0:T(8,128)S(1)}, f32[384,128]{1,0:T(8,128)S(1)}, u32[]{:S(2)}, u32[]{:S(2)}) %collective-permute-start.2) | collective-permute-done | bytes 196640 | tf_op jit(solution)/shard_map/ppermute | solution.py:83
  17.7 2.6 %collective-permute-start.3 = (f32[384,128]{1,0:T(8,128)S(1)}, f32[384,128]{1,0:T(8,128)S(1)}, u32[]{:S(2)}, u32[]{:S(2)}) collective-permute-start(f32[384,128]{1,0:T(8,128)S(1)} %add.22), channel_id=1, source_target_pairs={{0,8},{4,12},{8,0},{12,4},{1,9},{5,13},{9,1},{13,5},{2,10},{6,14},... | collective-permute-start | bytes 589832 | tf_op jit(solution)/shard_map/ppermute | solution.py:83
  20.3 8.1 %collective-permute-done.3 = f32[384,128]{1,0:T(8,128)S(1)} collective-permute-done((f32[384,128]{1,0:T(8,128)S(1)}, f32[384,128]{1,0:T(8,128)S(1)}, u32[]{:S(2)}, u32[]{:S(2)}) %collective-permute-start.3) | collective-permute-done | bytes 196640 | tf_op jit(solution)/shard_map/ppermute | solution.py:83
  28.4 0.1 copy.7
  28.5 0.0 copy-start
  28.5 0.7 %maximum_multiply_fusion.g_ref = f32[256,256]{1,0:T(8,128)} fusion(f32[128,128]{1,0:T(8,128)S(1)} %get-tuple-element.7, f32[128,128]{1,0:T(8,128)S(1)} %copy.7, f32[128,128]{1,0:T(8,128)S(1)} %get-tuple-element.8, f32[128,128]{1,0:T(8,128)S(1)} %get-tuple-element.5), kind=kLoop, calls=%fused_computation.12 | loop fusion | flops 262144 | bytes 524288 | tf_op jit(solution)/shard_map/div | solution.py:126
  29.3 15.0 %shard_map.17 = f32[32,256]{1,0:T(8,128)} custom-call(f32[256,256]{1,0:T(8,128)} %maximum_multiply_fusion.g_ref), custom_call_target="tpu_custom_call" | custom-call | tf_op jit(solution)/shard_map/pallas_call | solution.py:39
  44.3 0.0 copy-done
  44.3 0.0 copy-start.1
  44.3 1.0 %convolution_convert_fusion.1 = bf16[32,640]{1,0:T(8,128)(2,1)S(1)} fusion(bf16[640,256]{1,0:T(8,128)(2,1)S(1)} %copy-done, f32[32,256]{1,0:T(8,128)} %shard_map.17), kind=kOutput, calls=%fused_computation.4 | convolution fusion | flops 10514432 | bytes 401408 | tf_op jit(solution)/shard_map/dot_general | solution.py:128
  45.3 0.0 copy-done.1
  45.3 1.5 %fusion.1 = bf16[256,1,640]{2,0,1:T(8,128)(2,1)S(1)} fusion(bf16[32,640]{1,0:T(8,128)(2,1)S(1)} %convolution_convert_fusion.1, bf16[640,256]{1,0:T(8,128)(2,1)S(1)} %copy-done, s32[256]{0:T(256)S(1)} %iota_add_fusion, pred[256]{0:T(512)(128)(4,1)S(1)} %iota_compare_fusion, f32[32,256]{1,0:T(8,128)S(1)} %copy-done.1), kind=kOutput, calls=%fused_computation.3 | convolution fusion | flops 96215040 | bytes 730368 | tf_op jit(solution)/shard_map/dot_general | solution.py:133
  46.9 0.5 broadcast.27
  47.4 0.8 %reduce = bf16[256,640]{1,0:T(8,128)(2,1)S(1)} reduce(bf16[256,1,640]{2,0,1:T(8,128)(2,1)S(1)} %fusion.1, bf16[]{:T(256)} %broadcast.27), dimensions={1}, to_apply=%copy.8.reduce_sub_computation | reduce | bytes 655362 | tf_op jit(solution)/shard_map/broadcast_in_dim | solution.py:137
  48.2 0.1 reshape
  48.3 16.0 %all_to_all.18 = bf16[8,2,10240]{2,1,0:T(2,128)(2,1)S(1)} all-to-all(bf16[8,2,10240]{2,1,0:T(2,128)(2,1)S(1)} %reshape), channel_id=1, replica_groups=mesh['groups'=2,'pix'=4,'sub'=2,'inner'=2] {'pix','sub'}, dimensions={0} | all-to-all | bytes 655360 | tf_op jit(solution)/shard_map/all_to_all | solution.py:136
  64.3 0.3 reshape.1
  64.6 0.8 %copy.9 = bf16[32,8,640]{2,1,0:T(8,128)(2,1)} copy(bf16[32,8,640]{2,0,1:T(8,128)(2,1)S(1)} %bitcast.13) | data formatting | bytes 655360 | tf_op jit(solution)/shard_map/all_to_all | solution.py:136
  (11 shorter events, 0.2 us)
Async XLA Ops:
  1.4 1.6 %collective-permute-start = (f32[384,128]{1,0:T(8,128)S(1)}, f32[384,128]{1,0:T(8,128)S(1)}, u32[]{:S(2)}, u32[]{:S(2)}) collective-permute-start(f32[384,128]{1,0:T(8,128)S(1)} %pad_maximum_fusion), channel_id=1, source_target_pairs={{0,1},{1,0},{2,3},{3,2},{4,5},{5,4},{6,7},{7,6},{8,9},{9,8},{10,11... | collective-permute-start | bytes 589832 | tf_op jit(solution)/shard_map/ppermute | solution.py:83
  3.1 8.1 %collective-permute-start.1 = (f32[384,128]{1,0:T(8,128)S(1)}, f32[384,128]{1,0:T(8,128)S(1)}, u32[]{:S(2)}, u32[]{:S(2)}) collective-permute-start(f32[384,128]{1,0:T(8,128)S(1)} %fusion.21), channel_id=1, source_target_pairs={{0,2},{2,0},{1,3},{3,1},{4,6},{6,4},{5,7},{7,5},{8,10},{10,8},{9,1... | collective-permute-start | bytes 589832 | tf_op jit(solution)/shard_map/ppermute | solution.py:83
  11.2 6.4 %collective-permute-start.2 = (f32[384,128]{1,0:T(8,128)S(1)}, f32[384,128]{1,0:T(8,128)S(1)}, u32[]{:S(2)}, u32[]{:S(2)}) collective-permute-start(f32[384,128]{1,0:T(8,128)S(1)} %add.21), channel_id=1, source_target_pairs={{0,4},{4,0},{8,12},{12,8},{1,5},{5,1},{9,13},{13,9},{2,6},{6,2},{1... | collective-permute-start | bytes 589832 | tf_op jit(solution)/shard_map/ppermute | solution.py:83
  17.7 10.7 %collective-permute-start.3 = (f32[384,128]{1,0:T(8,128)S(1)}, f32[384,128]{1,0:T(8,128)S(1)}, u32[]{:S(2)}, u32[]{:S(2)}) collective-permute-start(f32[384,128]{1,0:T(8,128)S(1)} %add.22), channel_id=1, source_target_pairs={{0,8},{4,12},{8,0},{12,4},{1,9},{5,13},{9,1},{13,5},{2,10},{6,14},... | collective-permute-start | bytes 589832 | tf_op jit(solution)/shard_map/ppermute | solution.py:83
  28.5 15.8 %copy-start = (bf16[640,256]{1,0:T(8,128)(2,1)S(1)}, bf16[640,256]{1,0:T(8,128)(2,1)}, u32[]{:S(2)}) copy-start(bf16[640,256]{1,0:T(8,128)(2,1)} %param.1) | copy-start | bytes 983044
  44.3 1.0 %copy-start.1 = (f32[32,256]{1,0:T(8,128)S(1)}, f32[32,256]{1,0:T(8,128)}, u32[]{:S(2)}) copy-start(f32[32,256]{1,0:T(8,128)} %shard_map.17) | copy-start | bytes 98308

commit v3 on v2

v3 whole, which is shorter than its diff:
```python
import math

import jax
import jax.numpy as jnp
from jax import lax
from jax.experimental import pallas as pl
from jax.experimental.pallas import tpu as pltpu
from jax.sharding import PartitionSpec as P

MODES = 32
ITERS = 4
HI = lax.Precision.HIGHEST


def modes_kernel(g_ref, out_ref):
    g = g_ref[...]
    m = out_ref.shape[0]
    rows = lax.broadcasted_iota(jnp.int32, (m, 1), 0)
    cols = lax.broadcasted_iota(jnp.int32, (1, m), 1)
    xt = g[:m, :]
    for it in range(ITERS):
        pt = xt if it == 0 else jnp.dot(xt, g, precision=HI, preferred_element_type=jnp.float32)
        c = lax.dot_general(pt, pt, (((1,), (1,)), ((), ())), precision=HI,
                            preferred_element_type=jnp.float32)
        xt = pt
        for j in range(m):
            d = jnp.sqrt(c[j:j + 1, j:j + 1])
            q = xt[j:j + 1, :] / d
            rcol = jnp.where(rows > j, c[:, j:j + 1] / d, 0.0)
            rrow = jnp.where(cols > j, c[j:j + 1, :] / d, 0.0)
            xt = jnp.where(rows == j, q, xt - rcol * q)
            c = c - rcol * rrow
    out_ref[...] = xt


def leading_modes_t(gram):
    n = gram.shape[0]
    return pl.pallas_call(
        modes_kernel,
        out_shape=jax.ShapeDtypeStruct((MODES, n), jnp.float32),
        in_specs=[pl.BlockSpec(memory_space=pltpu.VMEM)],
        out_specs=pl.BlockSpec(memory_space=pltpu.VMEM),
    )(gram)


def delay_table(channels):
    middle = channels // 2
    row_index = lax.broadcasted_iota(jnp.int32, (channels, channels), 0)
    col_index = lax.broadcasted_iota(jnp.int32, (channels, channels), 1)
    harmonic = jnp.where(row_index <= middle, row_index, row_index - middle)
    angles = (harmonic * col_index % channels).astype(jnp.float32) * (2.0 * math.pi / channels)
    values = jnp.where(row_index <= middle, jnp.cos(angles), jnp.sin(angles)) / math.sqrt(channels)
    return values.astype(jnp.bfloat16)


def sym_pack(g):
    h = g.shape[0] // 2
    return jnp.concatenate([g[:h, :h], g[:h, h:], g[h:, h:]], axis=0)


def sym_unpack(packed):
    h = packed.shape[0] // 3
    a, b, d = packed[:h], packed[h:2 * h], packed[2 * h:]
    return jnp.concatenate([jnp.concatenate([a, b], 1), jnp.concatenate([b.T, d], 1)], 0)


def xor_perm(n, d):
    return [(i, i ^ d) for i in range(n)]


def halve(x, name, n, d):
    bit = (lax.axis_index(name) // d) % 2
    half = x.shape[0] // 2
    lo, hi = x[:half], x[half:]
    send = jnp.where(bit == 0, hi, lo)
    keep = jnp.where(bit == 0, lo, hi)
    return keep + lax.ppermute(send, name, xor_perm(n, d))


def double(x, name, n, d):
    bit = (lax.axis_index(name) // d) % 2
    other = lax.ppermute(x, name, xor_perm(n, d))
    return jnp.where(bit == 0, jnp.concatenate([x, other]), jnp.concatenate([other, x]))


def butterfly_sum(x, sizes):
    for name, n in sizes:
        d = 1
        while d < n:
            x = x + lax.ppermute(x, name, xor_perm(n, d))
            d *= 2
    return x


def gram_sum(g, mesh):
    n_in = mesh.shape["inner"]
    x = sym_pack(g)
    if n_in == 2:
        x = halve(x, "inner", 2, 1)
        x = butterfly_sum(x, [("sub", mesh.shape["sub"]), ("pix", mesh.shape["pix"])])
        x = double(x, "inner", 2, 1)
    else:
        x = butterfly_sum(x, [(a, mesh.shape[a]) for a in ("inner", "sub", "pix")])
    return sym_unpack(x)


def make_local(mesh):
    def local(cube):
        pixels, channels = cube.shape
        pixel_count = pixels * lax.axis_size(("pix", "sub", "inner"))
        partial_gram = lax.dot_general(
            cube, cube, (((0,), (0,)), ((), ())), preferred_element_type=jnp.float32
        )
        gram_matrix = gram_sum(partial_gram, mesh) / pixel_count
        modes_b = leading_modes_t(gram_matrix).T.astype(jnp.bfloat16)
        amplitudes = jnp.dot(cube, modes_b, preferred_element_type=jnp.float32).astype(jnp.bfloat16)
        cleaned = (cube - jnp.dot(amplitudes, modes_b.T, preferred_element_type=jnp.float32)).astype(
            jnp.bfloat16
        )
        table_b = delay_table(channels)
        coefficients = lax.dot_general(
            table_b, cleaned, (((1,), (1,)), ((), ())), preferred_element_type=jnp.float32
        ).astype(jnp.bfloat16)
        return lax.all_to_all(
            coefficients[:, None, :], ("pix", "sub"), split_axis=0, concat_axis=1, tiled=True
        )
    return local


def solution(mesh):
    return jax.shard_map(
        make_local(mesh),
        mesh=mesh,
        in_specs=(P(("groups", "pix", "sub", "inner"), None),),
        out_specs=P(("pix", "sub"), "groups", "inner"),
        check_vma=False,
    )
```

time: 65.7 us -> 60 us (0.913)
  waiting for transfers between devices: 18.9 us -> 10.8 us
  blocking collectives: 16 us -> 18 us
    ppermute x4 -> x5, waiting for transfers between devices: 18.9 us -> 10.8 us  [the longest x3 8.58 us: butterfly_sum(): x = x + lax.ppermute(x, name, xor_perm(n, d))]
    all_to_all x1, blocking collectives: 16 us -> 18 us  [local(): lax.all_to_all(coefficients[:, None, :], ('pix', 'sub'), split_axis=0, co...]
    ppermute x4 -> x5, starting transfers between devices: 7.98 us -> 8.32 us  [the longest x3 7.68 us: butterfly_sum(): x = x + lax.ppermute(x, name, xor_perm(n, d))]
  transfers between devices with their start and end apart: 4 -> 5, of which waited for: 4 -> 5; matrix products, arithmetic and copies ran while one was open for 0% -> 0% of each run, Pallas kernels for 0% -> 0%
where the time goes in v3:
time: 60 us; the launch traced here: 59.8 us
  blocking collectives  18 us (30%)
  Pallas kernels  15 us (25%)
  waiting for transfers between devices  10.8 us (18%)
  starting transfers between devices  8.32 us (14%)
  matrix products  3.91 us (7%)
  local copies, waits for them, and re-layouts  1.92 us (3%)
  other arithmetic  1.65 us (3%)
    all_to_all x1, blocking collectives, local(): lax.all_to_all(coefficients[:, None, :], ('pix', 'sub'), split_axis=0, co...  18 us
    pallas_call x1, Pallas kernels, leading_modes_t(): pl.pallas_call(modes_kernel, out_shape=jax.ShapeDtypeStruct((MODES, n), j...  15 us
    ppermute x3, waiting for transfers between devices, butterfly_sum(): x = x + lax.ppermute(x, name, xor_perm(n, d))  8.58 us
    ppermute x3, starting transfers between devices, butterfly_sum(): x = x + lax.ppermute(x, name, xor_perm(n, d))  7.68 us
    dot_general x1, matrix products, local(): lax.dot_general(table_b, cleaned, (((1,), (1,)), ((), ())), preferred_ele...  1.51 us
    dot_general x1, matrix products, local(): lax.dot_general(cube, cube, (((0,), (0,)), ((), ())), preferred_element_t...  1.37 us
    ppermute x1, waiting for transfers between devices, double(): other = lax.ppermute(x, name, xor_perm(n, d))  1.28 us
  transfers between devices with their start and end apart: 5, of which 5 were waited for; matrix products, arithmetic and copies ran while one was open for 0% of the time, Pallas kernels for 0%

profile of v3, /device:TPU:0, one launch (start us, length us, event | category | flops | bytes accessed | tf_op | source)
XLA Modules:
  0.0 59.8 jit_solution(3773909812199871555)
XLA Ops:
  0.0 1.4 %fusion.22 = f32[256,256]{1,0:T(8,128)S(1)} fusion(bf16[640,256]{1,0:T(8,128)(2,1)} %param.1), kind=kOutput, calls=%fused_computation.36 | convolution fusion | flops 83886080 | bytes 589824 | tf_op jit(solution)/shard_map/dot_general | solution.py:111
  1.4 0.6 collective-permute-start
  2.0 0.9 %collective-permute-done = f32[192,128]{1,0:T(8,128)S(1)} collective-permute-done((f32[192,128]{1,0:T(8,128)S(1)}, f32[192,128]{1,0:T(8,128)S(1)}, u32[]{:S(2)}, u32[]{:S(2)}) %collective-permute-start) | collective-permute-done | bytes 98336 | tf_op jit(solution)/shard_map/ppermute | solution.py:77
  3.0 2.9 %collective-permute-start.1 = (f32[192,128]{1,0:T(8,128)S(1)}, f32[192,128]{1,0:T(8,128)S(1)}, u32[]{:S(2)}, u32[]{:S(2)}) collective-permute-start(f32[192,128]{1,0:T(8,128)S(1)} %select_add_fusion), channel_id=1, source_target_pairs={{0,2},{2,0},{1,3},{3,1},{4,6},{6,4},{5,7},{7,5},{8,10},{10,8},{9,1... | collective-permute-start | bytes 294920 | tf_op jit(solution)/shard_map/ppermute | solution.py:90
  5.9 3.1 %collective-permute-done.1 = f32[192,128]{1,0:T(8,128)S(1)} collective-permute-done((f32[192,128]{1,0:T(8,128)S(1)}, f32[192,128]{1,0:T(8,128)S(1)}, u32[]{:S(2)}, u32[]{:S(2)}) %collective-permute-start.1) | collective-permute-done | bytes 98336 | tf_op jit(solution)/shard_map/ppermute | solution.py:90
  9.0 1.9 %collective-permute-start.2 = (f32[192,128]{1,0:T(8,128)S(1)}, f32[192,128]{1,0:T(8,128)S(1)}, u32[]{:S(2)}, u32[]{:S(2)}) collective-permute-start(f32[192,128]{1,0:T(8,128)S(1)} %add.28), channel_id=1, source_target_pairs={{0,4},{4,0},{8,12},{12,8},{1,5},{5,1},{9,13},{13,9},{2,6},{6,2},{1... | collective-permute-start | bytes 294920 | tf_op jit(solution)/shard_map/ppermute | solution.py:90
  10.9 2.8 %collective-permute-done.2 = f32[192,128]{1,0:T(8,128)S(1)} collective-permute-done((f32[192,128]{1,0:T(8,128)S(1)}, f32[192,128]{1,0:T(8,128)S(1)}, u32[]{:S(2)}, u32[]{:S(2)}) %collective-permute-start.2) | collective-permute-done | bytes 98336 | tf_op jit(solution)/shard_map/ppermute | solution.py:90
  13.7 2.9 %collective-permute-start.3 = (f32[192,128]{1,0:T(8,128)S(1)}, f32[192,128]{1,0:T(8,128)S(1)}, u32[]{:S(2)}, u32[]{:S(2)}) collective-permute-start(f32[192,128]{1,0:T(8,128)S(1)} %add.29), channel_id=1, source_target_pairs={{0,8},{4,12},{8,0},{12,4},{1,9},{5,13},{9,1},{13,5},{2,10},{6,14},... | collective-permute-start | bytes 294920 | tf_op jit(solution)/shard_map/ppermute | solution.py:90
  16.6 2.7 %collective-permute-done.3 = f32[192,128]{1,0:T(8,128)S(1)} collective-permute-done((f32[192,128]{1,0:T(8,128)S(1)}, f32[192,128]{1,0:T(8,128)S(1)}, u32[]{:S(2)}, u32[]{:S(2)}) %collective-permute-start.3) | collective-permute-done | bytes 98336 | tf_op jit(solution)/shard_map/ppermute | solution.py:90
  19.3 0.1 collective-permute-start.4
  19.4 1.3 %collective-permute-done.4 = f32[192,128]{1,0:T(8,128)S(1)} collective-permute-done((f32[192,128]{1,0:T(8,128)S(1)}, f32[192,128]{1,0:T(8,128)S(1)}, u32[]{:S(2)}, u32[]{:S(2)}) %collective-permute-start.4) | collective-permute-done | bytes 98336 | tf_op jit(solution)/shard_map/ppermute | solution.py:82
  20.7 0.1 copy.7
  20.8 0.0 copy-start
  20.8 0.7 %maximum_multiply_fusion.g_ref = f32[256,256]{1,0:T(8,128)} fusion(f32[128,128]{1,0:T(8,128)S(1)} %get-tuple-element.7, f32[128,128]{1,0:T(8,128)S(1)} %copy.7, f32[128,128]{1,0:T(8,128)S(1)} %get-tuple-element.8, f32[128,128]{1,0:T(8,128)S(1)} %get-tuple-element.5), kind=kLoop, calls=%fused_computation.12 | loop fusion | flops 262144 | bytes 524288 | tf_op jit(solution)/shard_map/div | solution.py:114
  21.5 15.0 %shard_map.17 = f32[32,256]{1,0:T(8,128)} custom-call(f32[256,256]{1,0:T(8,128)} %maximum_multiply_fusion.g_ref), custom_call_target="tpu_custom_call" | custom-call | tf_op jit(solution)/shard_map/pallas_call | solution.py:38
  36.6 0.0 copy-done
  36.6 0.0 copy-start.1
  36.6 1.0 %convolution_convert_fusion.1 = bf16[32,640]{1,0:T(8,128)(2,1)S(1)} fusion(bf16[640,256]{1,0:T(8,128)(2,1)S(1)} %copy-done, f32[32,256]{1,0:T(8,128)} %shard_map.17), kind=kOutput, calls=%fused_computation.4 | convolution fusion | flops 10514432 | bytes 401408 | tf_op jit(solution)/shard_map/dot_general | solution.py:116
  37.6 0.0 copy-done.1
  37.6 1.5 %fusion.1 = bf16[256,1,640]{2,0,1:T(8,128)(2,1)S(1)} fusion(bf16[32,640]{1,0:T(8,128)(2,1)S(1)} %convolution_convert_fusion.1, bf16[640,256]{1,0:T(8,128)(2,1)S(1)} %copy-done, s32[256]{0:T(256)S(1)} %iota_add_fusion, pred[256]{0:T(512)(128)(4,1)S(1)} %iota_compare_fusion, f32[32,256]{1,0:T(8,128)S(1)} %copy-done.1), kind=kOutput, calls=%fused_computation.3 | convolution fusion | flops 96215040 | bytes 730368 | tf_op jit(solution)/shard_map/dot_general | solution.py:121
  39.1 0.5 broadcast.29
  39.6 0.8 %reduce = bf16[256,640]{1,0:T(8,128)(2,1)S(1)} reduce(bf16[256,1,640]{2,0,1:T(8,128)(2,1)S(1)} %fusion.1, bf16[]{:T(256)} %broadcast.29), dimensions={1}, to_apply=%copy.8.reduce_sub_computation | reduce | bytes 655362 | tf_op jit(solution)/shard_map/broadcast_in_dim | solution.py:125
  40.5 0.1 reshape
  40.6 18.0 %all_to_all.18 = bf16[8,2,10240]{2,1,0:T(2,128)(2,1)S(1)} all-to-all(bf16[8,2,10240]{2,1,0:T(2,128)(2,1)S(1)} %reshape), channel_id=1, replica_groups=mesh['groups'=2,'pix'=4,'sub'=2,'inner'=2] {'pix','sub'}, dimensions={0} | all-to-all | bytes 655360 | tf_op jit(solution)/shard_map/all_to_all | solution.py:124
  58.6 0.3 reshape.1
  58.9 0.8 %copy.9 = bf16[32,8,640]{2,1,0:T(8,128)(2,1)} copy(bf16[32,8,640]{2,0,1:T(8,128)(2,1)S(1)} %bitcast.13) | data formatting | bytes 655360 | tf_op jit(solution)/shard_map/all_to_all | solution.py:124
  (12 shorter events, 0.2 us)
Async XLA Ops:
  1.4 1.5 %collective-permute-start = (f32[192,128]{1,0:T(8,128)S(1)}, f32[192,128]{1,0:T(8,128)S(1)}, u32[]{:S(2)}, u32[]{:S(2)}) collective-permute-start(f32[192,128]{1,0:T(8,128)S(1)} %slice_select_fusion), channel_id=1, source_target_pairs={{0,1},{1,0},{2,3},{3,2},{4,5},{5,4},{6,7},{7,6},{8,9},{9,8},{10,11... | collective-permute-start | bytes 294920 | tf_op jit(solution)/shard_map/ppermute | solution.py:77
  3.0 6.0 %collective-permute-start.1 = (f32[192,128]{1,0:T(8,128)S(1)}, f32[192,128]{1,0:T(8,128)S(1)}, u32[]{:S(2)}, u32[]{:S(2)}) collective-permute-start(f32[192,128]{1,0:T(8,128)S(1)} %select_add_fusion), channel_id=1, source_target_pairs={{0,2},{2,0},{1,3},{3,1},{4,6},{6,4},{5,7},{7,5},{8,10},{10,8},{9,1... | collective-permute-start | bytes 294920 | tf_op jit(solution)/shard_map/ppermute | solution.py:90
  9.0 4.7 %collective-permute-start.2 = (f32[192,128]{1,0:T(8,128)S(1)}, f32[192,128]{1,0:T(8,128)S(1)}, u32[]{:S(2)}, u32[]{:S(2)}) collective-permute-start(f32[192,128]{1,0:T(8,128)S(1)} %add.28), channel_id=1, source_target_pairs={{0,4},{4,0},{8,12},{12,8},{1,5},{5,1},{9,13},{13,9},{2,6},{6,2},{1... | collective-permute-start | bytes 294920 | tf_op jit(solution)/shard_map/ppermute | solution.py:90
  13.7 5.6 %collective-permute-start.3 = (f32[192,128]{1,0:T(8,128)S(1)}, f32[192,128]{1,0:T(8,128)S(1)}, u32[]{:S(2)}, u32[]{:S(2)}) collective-permute-start(f32[192,128]{1,0:T(8,128)S(1)} %add.29), channel_id=1, source_target_pairs={{0,8},{4,12},{8,0},{12,4},{1,9},{5,13},{9,1},{13,5},{2,10},{6,14},... | collective-permute-start | bytes 294920 | tf_op jit(solution)/shard_map/ppermute | solution.py:90
  19.3 1.4 %collective-permute-start.4 = (f32[192,128]{1,0:T(8,128)S(1)}, f32[192,128]{1,0:T(8,128)S(1)}, u32[]{:S(2)}, u32[]{:S(2)}) collective-permute-start(f32[192,128]{1,0:T(8,128)S(1)} %add.30), channel_id=1, source_target_pairs={{0,1},{1,0},{2,3},{3,2},{4,5},{5,4},{6,7},{7,6},{8,9},{9,8},{10,11... | collective-permute-start | bytes 294920 | tf_op jit(solution)/shard_map/ppermute | solution.py:82
  20.8 15.8 %copy-start = (bf16[640,256]{1,0:T(8,128)(2,1)S(1)}, bf16[640,256]{1,0:T(8,128)(2,1)}, u32[]{:S(2)}) copy-start(bf16[640,256]{1,0:T(8,128)(2,1)} %param.1) | copy-start | bytes 983044
  36.6 1.0 %copy-start.1 = (f32[32,256]{1,0:T(8,128)S(1)}, f32[32,256]{1,0:T(8,128)}, u32[]{:S(2)}) copy-start(f32[32,256]{1,0:T(8,128)} %shard_map.17) | copy-start | bytes 98308

commit v4 on v3

--- a/solution.py
+++ b/solution.py
@@ -121,9 +121,10 @@
         coefficients = lax.dot_general(
             table_b, cleaned, (((1,), (1,)), ((), ())), preferred_element_type=jnp.float32
         ).astype(jnp.bfloat16)
-        return lax.all_to_all(
-            coefficients[:, None, :], ("pix", "sub"), split_axis=0, concat_axis=1, tiled=True
-        )
+        k = lax.axis_size(("pix", "sub"))
+        blocks = coefficients.reshape(k, coefficients.shape[0] // k, coefficients.shape[1])
+        blocks = lax.all_to_all(blocks, ("pix", "sub"), split_axis=0, concat_axis=0, tiled=True)
+        return jnp.transpose(blocks, (1, 0, 2))
     return local
 
 

time: 60 us -> 58.2 us (0.970)
  local copies, waits for them, and re-layouts: 1.92 us -> 0.96 us
  other arithmetic: 1.65 us -> 0.83 us
    all_to_all x1 -> x0, local copies, waits for them, and re-layouts: 0.83 us -> none  [local(): lax.all_to_all(coefficients[:, None, :], ('pix', 'sub'), split_axis=0, co...]
    transpose x0 -> x1, local copies, waits for them, and re-layouts: none -> 0.83 us  [local(): return jnp.transpose(blocks, (1, 0, 2))]
    broadcast_in_dim x1 -> x0, other arithmetic: 0.82 us -> none  [local(): coefficients[:, None, :]]
where the time goes in v4:
time: 58.2 us; the launch traced here: 58 us
  blocking collectives  18 us (31%)
  Pallas kernels  15 us (26%)
  waiting for transfers between devices  10.8 us (19%)
  starting transfers between devices  8.32 us (14%)
  matrix products  3.91 us (7%)
  local copies, waits for them, and re-layouts  0.96 us (2%)
  other arithmetic  0.83 us (1%)
    all_to_all x1, blocking collectives, local(): lax.all_to_all(blocks, ('pix', 'sub'), split_axis=0, concat_axis=0, tiled...  18 us
    pallas_call x1, Pallas kernels, leading_modes_t(): pl.pallas_call(modes_kernel, out_shape=jax.ShapeDtypeStruct((MODES, n), j...  15 us
    ppermute x3, waiting for transfers between devices, butterfly_sum(): x = x + lax.ppermute(x, name, xor_perm(n, d))  8.58 us
    ppermute x3, starting transfers between devices, butterfly_sum(): x = x + lax.ppermute(x, name, xor_perm(n, d))  7.68 us
    dot_general x1, matrix products, local(): lax.dot_general(table_b, cleaned, (((1,), (1,)), ((), ())), preferred_ele...  1.51 us
    dot_general x1, matrix products, local(): lax.dot_general(cube, cube, (((0,), (0,)), ((), ())), preferred_element_t...  1.37 us
    ppermute x1, waiting for transfers between devices, double(): other = lax.ppermute(x, name, xor_perm(n, d))  1.28 us
  transfers between devices with their start and end apart: 5, of which 5 were waited for; matrix products, arithmetic and copies ran while one was open for 0% of the time, Pallas kernels for 0%

profile of v4, /device:TPU:0, one launch (start us, length us, event | category | flops | bytes accessed | tf_op | source)
XLA Modules:
  0.0 58.0 jit_solution(14374894636723488737)
XLA Ops:
  0.0 1.4 %fusion.21 = f32[256,256]{1,0:T(8,128)S(1)} fusion(bf16[640,256]{1,0:T(8,128)(2,1)} %param.1), kind=kOutput, calls=%fused_computation.35 | convolution fusion | flops 83886080 | bytes 589824 | tf_op jit(solution)/shard_map/dot_general | solution.py:111
  1.4 0.6 collective-permute-start
  2.0 0.9 %collective-permute-done = f32[192,128]{1,0:T(8,128)S(1)} collective-permute-done((f32[192,128]{1,0:T(8,128)S(1)}, f32[192,128]{1,0:T(8,128)S(1)}, u32[]{:S(2)}, u32[]{:S(2)}) %collective-permute-start) | collective-permute-done | bytes 98336 | tf_op jit(solution)/shard_map/ppermute | solution.py:77
  3.0 2.9 %collective-permute-start.1 = (f32[192,128]{1,0:T(8,128)S(1)}, f32[192,128]{1,0:T(8,128)S(1)}, u32[]{:S(2)}, u32[]{:S(2)}) collective-permute-start(f32[192,128]{1,0:T(8,128)S(1)} %select_add_fusion), channel_id=1, source_target_pairs={{0,2},{2,0},{1,3},{3,1},{4,6},{6,4},{5,7},{7,5},{8,10},{10,8},{9,1... | collective-permute-start | bytes 294920 | tf_op jit(solution)/shard_map/ppermute | solution.py:90
  5.9 3.1 %collective-permute-done.1 = f32[192,128]{1,0:T(8,128)S(1)} collective-permute-done((f32[192,128]{1,0:T(8,128)S(1)}, f32[192,128]{1,0:T(8,128)S(1)}, u32[]{:S(2)}, u32[]{:S(2)}) %collective-permute-start.1) | collective-permute-done | bytes 98336 | tf_op jit(solution)/shard_map/ppermute | solution.py:90
  9.0 1.9 %collective-permute-start.2 = (f32[192,128]{1,0:T(8,128)S(1)}, f32[192,128]{1,0:T(8,128)S(1)}, u32[]{:S(2)}, u32[]{:S(2)}) collective-permute-start(f32[192,128]{1,0:T(8,128)S(1)} %add.28), channel_id=1, source_target_pairs={{0,4},{4,0},{8,12},{12,8},{1,5},{5,1},{9,13},{13,9},{2,6},{6,2},{1... | collective-permute-start | bytes 294920 | tf_op jit(solution)/shard_map/ppermute | solution.py:90
  10.9 2.8 %collective-permute-done.2 = f32[192,128]{1,0:T(8,128)S(1)} collective-permute-done((f32[192,128]{1,0:T(8,128)S(1)}, f32[192,128]{1,0:T(8,128)S(1)}, u32[]{:S(2)}, u32[]{:S(2)}) %collective-permute-start.2) | collective-permute-done | bytes 98336 | tf_op jit(solution)/shard_map/ppermute | solution.py:90
  13.7 2.9 %collective-permute-start.3 = (f32[192,128]{1,0:T(8,128)S(1)}, f32[192,128]{1,0:T(8,128)S(1)}, u32[]{:S(2)}, u32[]{:S(2)}) collective-permute-start(f32[192,128]{1,0:T(8,128)S(1)} %add.29), channel_id=1, source_target_pairs={{0,8},{4,12},{8,0},{12,4},{1,9},{5,13},{9,1},{13,5},{2,10},{6,14},... | collective-permute-start | bytes 294920 | tf_op jit(solution)/shard_map/ppermute | solution.py:90
  16.6 2.7 %collective-permute-done.3 = f32[192,128]{1,0:T(8,128)S(1)} collective-permute-done((f32[192,128]{1,0:T(8,128)S(1)}, f32[192,128]{1,0:T(8,128)S(1)}, u32[]{:S(2)}, u32[]{:S(2)}) %collective-permute-start.3) | collective-permute-done | bytes 98336 | tf_op jit(solution)/shard_map/ppermute | solution.py:90
  19.3 0.1 collective-permute-start.4
  19.4 1.3 %collective-permute-done.4 = f32[192,128]{1,0:T(8,128)S(1)} collective-permute-done((f32[192,128]{1,0:T(8,128)S(1)}, f32[192,128]{1,0:T(8,128)S(1)}, u32[]{:S(2)}, u32[]{:S(2)}) %collective-permute-start.4) | collective-permute-done | bytes 98336 | tf_op jit(solution)/shard_map/ppermute | solution.py:82
  20.7 0.1 copy.4
  20.8 0.0 copy-start
  20.8 0.7 %maximum_multiply_fusion.g_ref = f32[256,256]{1,0:T(8,128)} fusion(f32[128,128]{1,0:T(8,128)S(1)} %get-tuple-element.7, f32[128,128]{1,0:T(8,128)S(1)} %copy.4, f32[128,128]{1,0:T(8,128)S(1)} %get-tuple-element.8, f32[128,128]{1,0:T(8,128)S(1)} %get-tuple-element.5), kind=kLoop, calls=%fused_computation.11 | loop fusion | flops 262144 | bytes 524288 | tf_op jit(solution)/shard_map/div | solution.py:114
  21.5 15.0 %shard_map.17 = f32[32,256]{1,0:T(8,128)} custom-call(f32[256,256]{1,0:T(8,128)} %maximum_multiply_fusion.g_ref), custom_call_target="tpu_custom_call" | custom-call | tf_op jit(solution)/shard_map/pallas_call | solution.py:38
  36.6 0.0 copy-done
  36.6 0.0 copy-start.1
  36.6 1.0 %convolution_convert_fusion.1 = bf16[32,640]{1,0:T(8,128)(2,1)S(1)} fusion(bf16[640,256]{1,0:T(8,128)(2,1)S(1)} %copy-done, f32[32,256]{1,0:T(8,128)} %shard_map.17), kind=kOutput, calls=%fused_computation.3 | convolution fusion | flops 10514432 | bytes 401408 | tf_op jit(solution)/shard_map/dot_general | solution.py:116
  37.6 0.0 copy-done.1
  37.6 1.5 %convolution_convert_fusion = bf16[256,640]{1,0:T(8,128)(2,1)S(1)} fusion(bf16[32,640]{1,0:T(8,128)(2,1)S(1)} %convolution_convert_fusion.1, bf16[640,256]{1,0:T(8,128)(2,1)S(1)} %copy-done, s32[256]{0:T(256)S(1)} %iota_add_fusion, pred[256]{0:T(512)(128)(4,1)S(1)} %iota_compare_fusion, f32[32,256]{1,0:T(8,128)S(1)} %copy-done.1), kind=kOutput, calls=%fused_computation.1 | convolution fusion | flops 96215040 | bytes 730368 | tf_op jit(solution)/shard_map/dot_general | solution.py:121
  39.1 18.0 %all_to_all.5 = bf16[8,32,640]{2,1,0:T(8,128)(2,1)S(1)} all-to-all(bf16[8,32,640]{2,1,0:T(8,128)(2,1)S(1)} %bitcast.9), channel_id=1, replica_groups=mesh['groups'=2,'pix'=4,'sub'=2,'inner'=2] {'pix','sub'}, dimensions={0} | all-to-all | bytes 655360 | tf_op jit(solution)/shard_map/all_to_all | solution.py:126
  57.1 0.8 %copy.5 = bf16[32,8,640]{2,1,0:T(8,128)(2,1)} copy(bf16[32,8,640]{2,0,1:T(8,128)(2,1)S(1)} %bitcast.8) | data formatting | bytes 655360 | tf_op jit(solution)/shard_map/transpose | solution.py:127
  (11 shorter events, 0.1 us)
Async XLA Ops:
  1.4 1.5 %collective-permute-start = (f32[192,128]{1,0:T(8,128)S(1)}, f32[192,128]{1,0:T(8,128)S(1)}, u32[]{:S(2)}, u32[]{:S(2)}) collective-permute-start(f32[192,128]{1,0:T(8,128)S(1)} %slice_select_fusion), channel_id=1, source_target_pairs={{0,1},{1,0},{2,3},{3,2},{4,5},{5,4},{6,7},{7,6},{8,9},{9,8},{10,11... | collective-permute-start | bytes 294920 | tf_op jit(solution)/shard_map/ppermute | solution.py:77
  3.0 6.0 %collective-permute-start.1 = (f32[192,128]{1,0:T(8,128)S(1)}, f32[192,128]{1,0:T(8,128)S(1)}, u32[]{:S(2)}, u32[]{:S(2)}) collective-permute-start(f32[192,128]{1,0:T(8,128)S(1)} %select_add_fusion), channel_id=1, source_target_pairs={{0,2},{2,0},{1,3},{3,1},{4,6},{6,4},{5,7},{7,5},{8,10},{10,8},{9,1... | collective-permute-start | bytes 294920 | tf_op jit(solution)/shard_map/ppermute | solution.py:90
  9.0 4.7 %collective-permute-start.2 = (f32[192,128]{1,0:T(8,128)S(1)}, f32[192,128]{1,0:T(8,128)S(1)}, u32[]{:S(2)}, u32[]{:S(2)}) collective-permute-start(f32[192,128]{1,0:T(8,128)S(1)} %add.28), channel_id=1, source_target_pairs={{0,4},{4,0},{8,12},{12,8},{1,5},{5,1},{9,13},{13,9},{2,6},{6,2},{1... | collective-permute-start | bytes 294920 | tf_op jit(solution)/shard_map/ppermute | solution.py:90
  13.7 5.6 %collective-permute-start.3 = (f32[192,128]{1,0:T(8,128)S(1)}, f32[192,128]{1,0:T(8,128)S(1)}, u32[]{:S(2)}, u32[]{:S(2)}) collective-permute-start(f32[192,128]{1,0:T(8,128)S(1)} %add.29), channel_id=1, source_target_pairs={{0,8},{4,12},{8,0},{12,4},{1,9},{5,13},{9,1},{13,5},{2,10},{6,14},... | collective-permute-start | bytes 294920 | tf_op jit(solution)/shard_map/ppermute | solution.py:90
  19.3 1.4 %collective-permute-start.4 = (f32[192,128]{1,0:T(8,128)S(1)}, f32[192,128]{1,0:T(8,128)S(1)}, u32[]{:S(2)}, u32[]{:S(2)}) collective-permute-start(f32[192,128]{1,0:T(8,128)S(1)} %add.30), channel_id=1, source_target_pairs={{0,1},{1,0},{2,3},{3,2},{4,5},{5,4},{6,7},{7,6},{8,9},{9,8},{10,11... | collective-permute-start | bytes 294920 | tf_op jit(solution)/shard_map/ppermute | solution.py:82
  20.8 15.8 %copy-start = (bf16[640,256]{1,0:T(8,128)(2,1)S(1)}, bf16[640,256]{1,0:T(8,128)(2,1)}, u32[]{:S(2)}) copy-start(bf16[640,256]{1,0:T(8,128)(2,1)} %param.1) | copy-start | bytes 983044
  36.6 1.0 %copy-start.1 = (f32[32,256]{1,0:T(8,128)S(1)}, f32[32,256]{1,0:T(8,128)}, u32[]{:S(2)}) copy-start(f32[32,256]{1,0:T(8,128)} %shard_map.17) | copy-start | bytes 98308

commit v5 on v4

--- a/solution.py
+++ b/solution.py
@@ -92,12 +92,41 @@
     return x
 
 
+def butterfly_steps(sizes):
+    steps = []
+    for name, n in sizes:
+        d = 1
+        while d < n:
+            steps.append((name, n, d))
+            d *= 2
+    return steps
+
+
+def paired_round(x, first, second, order):
+    (a1, n1, d1), (a2, n2, d2) = first, second
+    r1 = lax.ppermute(x, a1, xor_perm(n1, d1))
+    r2 = lax.ppermute(x, a2, xor_perm(n2, d2))
+    if a1 == a2:
+        r12 = lax.ppermute(x, a1, xor_perm(n1, d1 | d2))
+    else:
+        if order.index(a1) > order.index(a2):
+            a1, n1, d1, a2, n2, d2 = a2, n2, d2, a1, n1, d1
+        pairs = [(i * n2 + k, (i ^ d1) * n2 + (k ^ d2)) for i in range(n1) for k in range(n2)]
+        r12 = lax.ppermute(x, (a1, a2), pairs)
+    return (x + r1) + (r2 + r12)
+
+
 def gram_sum(g, mesh):
     n_in = mesh.shape["inner"]
     x = sym_pack(g)
     if n_in == 2:
         x = halve(x, "inner", 2, 1)
-        x = butterfly_sum(x, [("sub", mesh.shape["sub"]), ("pix", mesh.shape["pix"])])
+        steps = butterfly_steps([("sub", mesh.shape["sub"]), ("pix", mesh.shape["pix"])])
+        if len(steps) >= 2:
+            x = paired_round(x, steps[0], steps[1], list(mesh.axis_names))
+            steps = steps[2:]
+        for name, n, d in steps:
+            x = x + lax.ppermute(x, name, xor_perm(n, d))
         x = double(x, "inner", 2, 1)
     else:
         x = butterfly_sum(x, [(a, mesh.shape[a]) for a in ("inner", "sub", "pix")])

time: 58.2 us -> 56.9 us (0.978)
  blocking collectives: 18 us -> 16.3 us
  waiting for transfers between devices: 10.8 us -> 11.7 us
    all_to_all x1, blocking collectives: 18 us -> 16.3 us  [local(): lax.all_to_all(blocks, ('pix', 'sub'), split_axis=0, concat_axis=0, tiled...]
    ppermute x3 -> x4, waiting for transfers between devices: 8.58 us -> 9.49 us  [the longest x1 3.98 us: gram_sum(): x = x + lax.ppermute(x, name, xor_perm(n, d))]
    ppermute x3 -> x4, starting transfers between devices: 7.68 us -> 7.12 us  [the longest x1 2.89 us: paired_round(): r1 = lax.ppermute(x, a1, xor_perm(n1, d1))]
  transfers between devices with their start and end apart: 5 -> 6, of which waited for: 5 -> 6; matrix products, arithmetic and copies ran while one was open for 0% -> 0% of each run, Pallas kernels for 0% -> 0%
where the time goes in v5:
time: 56.9 us; the launch traced here: 56.6 us
  blocking collectives  16.3 us (29%)
  Pallas kernels  15 us (26%)
  waiting for transfers between devices  11.7 us (21%)
  starting transfers between devices  7.76 us (14%)
  matrix products  3.91 us (7%)
  local copies, waits for them, and re-layouts  0.96 us (2%)
  other arithmetic  0.82 us (1%)
    all_to_all x1, blocking collectives, local(): lax.all_to_all(blocks, ('pix', 'sub'), split_axis=0, concat_axis=0, tiled...  16.3 us
    pallas_call x1, Pallas kernels, leading_modes_t(): pl.pallas_call(modes_kernel, out_shape=jax.ShapeDtypeStruct((MODES, n), j...  15 us
    ppermute x1, waiting for transfers between devices, gram_sum(): x = x + lax.ppermute(x, name, xor_perm(n, d))  3.98 us
    ppermute x1, starting transfers between devices, paired_round(): r1 = lax.ppermute(x, a1, xor_perm(n1, d1))  2.89 us
    ppermute x1, starting transfers between devices, gram_sum(): x = x + lax.ppermute(x, name, xor_perm(n, d))  2.65 us
    ppermute x1, waiting for transfers between devices, paired_round(): r2 = lax.ppermute(x, a2, xor_perm(n2, d2))  2.38 us
    ppermute x1, waiting for transfers between devices, paired_round(): r12 = lax.ppermute(x, (a1, a2), pairs)  1.6 us
    ppermute x1, starting transfers between devices, paired_round(): r2 = lax.ppermute(x, a2, xor_perm(n2, d2))  1.58 us
  transfers between devices with their start and end apart: 6, of which 6 were waited for; matrix products, arithmetic and copies ran while one was open for 0% of the time, Pallas kernels for 0%

profile of v5, /device:TPU:0, one launch (start us, length us, event | category | flops | bytes accessed | tf_op | source)
XLA Modules:
  0.0 56.6 jit_solution(3001131109915360646)
XLA Ops:
  0.0 1.4 %fusion.21 = f32[256,256]{1,0:T(8,128)S(1)} fusion(bf16[640,256]{1,0:T(8,128)(2,1)} %param.1), kind=kOutput, calls=%fused_computation.36 | convolution fusion | flops 83886080 | bytes 589824 | tf_op jit(solution)/shard_map/dot_general | solution.py:140
  1.4 0.6 collective-permute-start
  2.0 0.9 %collective-permute-done = f32[192,128]{1,0:T(8,128)S(1)} collective-permute-done((f32[192,128]{1,0:T(8,128)S(1)}, f32[192,128]{1,0:T(8,128)S(1)}, u32[]{:S(2)}, u32[]{:S(2)}) %collective-permute-start) | collective-permute-done | bytes 98336 | tf_op jit(solution)/shard_map/ppermute | solution.py:77
  3.0 2.9 %collective-permute-start.1 = (f32[192,128]{1,0:T(8,128)S(1)}, f32[192,128]{1,0:T(8,128)S(1)}, u32[]{:S(2)}, u32[]{:S(2)}) collective-permute-start(f32[192,128]{1,0:T(8,128)S(1)} %select_add_fusion), channel_id=1, source_target_pairs={{0,2},{2,0},{1,3},{3,1},{4,6},{6,4},{5,7},{7,5},{8,10},{10,8},{9,1... | collective-permute-start | bytes 294920 | tf_op jit(solution)/shard_map/ppermute | solution.py:107
  5.9 1.6 %collective-permute-start.2 = (f32[192,128]{1,0:T(8,128)S(1)}, f32[192,128]{1,0:T(8,128)S(1)}, u32[]{:S(2)}, u32[]{:S(2)}) collective-permute-start(f32[192,128]{1,0:T(8,128)S(1)} %select_add_fusion), channel_id=1, source_target_pairs={{0,4},{4,0},{8,12},{12,8},{1,5},{5,1},{9,13},{13,9},{2,6},{6,2},{1... | collective-permute-start | bytes 294920 | tf_op jit(solution)/shard_map/ppermute | solution.py:108
  7.4 0.0 collective-permute-start.3
  7.4 1.5 %collective-permute-done.1 = f32[192,128]{1,0:T(8,128)S(1)} collective-permute-done((f32[192,128]{1,0:T(8,128)S(1)}, f32[192,128]{1,0:T(8,128)S(1)}, u32[]{:S(2)}, u32[]{:S(2)}) %collective-permute-start.1) | collective-permute-done | bytes 98336 | tf_op jit(solution)/shard_map/ppermute | solution.py:107
  9.0 2.4 %collective-permute-done.2 = f32[192,128]{1,0:T(8,128)S(1)} collective-permute-done((f32[192,128]{1,0:T(8,128)S(1)}, f32[192,128]{1,0:T(8,128)S(1)}, u32[]{:S(2)}, u32[]{:S(2)}) %collective-permute-start.2) | collective-permute-done | bytes 98336 | tf_op jit(solution)/shard_map/ppermute | solution.py:108
  11.4 1.6 %collective-permute-done.3 = f32[192,128]{1,0:T(8,128)S(1)} collective-permute-done((f32[192,128]{1,0:T(8,128)S(1)}, f32[192,128]{1,0:T(8,128)S(1)}, u32[]{:S(2)}, u32[]{:S(2)}) %collective-permute-start.3) | collective-permute-done | bytes 98336 | tf_op jit(solution)/shard_map/ppermute | solution.py:115
  13.0 2.7 %collective-permute-start.4 = (f32[192,128]{1,0:T(8,128)S(1)}, f32[192,128]{1,0:T(8,128)S(1)}, u32[]{:S(2)}, u32[]{:S(2)}) collective-permute-start(f32[192,128]{1,0:T(8,128)S(1)} %add_add_fusion), channel_id=1, source_target_pairs={{0,8},{4,12},{8,0},{12,4},{1,9},{5,13},{9,1},{13,5},{2,10},{6,14},... | collective-permute-start | bytes 294920 | tf_op jit(solution)/shard_map/ppermute | solution.py:129
  15.6 4.0 %collective-permute-done.4 = f32[192,128]{1,0:T(8,128)S(1)} collective-permute-done((f32[192,128]{1,0:T(8,128)S(1)}, f32[192,128]{1,0:T(8,128)S(1)}, u32[]{:S(2)}, u32[]{:S(2)}) %collective-permute-start.4) | collective-permute-done | bytes 98336 | tf_op jit(solution)/shard_map/ppermute | solution.py:129
  19.6 0.1 collective-permute-start.5
  19.7 1.3 %collective-permute-done.5 = f32[192,128]{1,0:T(8,128)S(1)} collective-permute-done((f32[192,128]{1,0:T(8,128)S(1)}, f32[192,128]{1,0:T(8,128)S(1)}, u32[]{:S(2)}, u32[]{:S(2)}) %collective-permute-start.5) | collective-permute-done | bytes 98336 | tf_op jit(solution)/shard_map/ppermute | solution.py:82
  21.1 0.1 copy.4
  21.1 0.0 copy-start
  21.2 0.7 %maximum_multiply_fusion.g_ref = f32[256,256]{1,0:T(8,128)} fusion(f32[128,128]{1,0:T(8,128)S(1)} %get-tuple-element.7, f32[128,128]{1,0:T(8,128)S(1)} %copy.4, f32[128,128]{1,0:T(8,128)S(1)} %get-tuple-element.8, f32[128,128]{1,0:T(8,128)S(1)} %get-tuple-element.5), kind=kLoop, calls=%fused_computation.11 | loop fusion | flops 262144 | bytes 524288 | tf_op jit(solution)/shard_map/div | solution.py:143
  21.9 15.0 %shard_map.17 = f32[32,256]{1,0:T(8,128)} custom-call(f32[256,256]{1,0:T(8,128)} %maximum_multiply_fusion.g_ref), custom_call_target="tpu_custom_call" | custom-call | tf_op jit(solution)/shard_map/pallas_call | solution.py:38
  36.9 0.0 copy-done
  36.9 0.0 copy-start.1
  36.9 1.0 %convolution_convert_fusion.1 = bf16[32,640]{1,0:T(8,128)(2,1)S(1)} fusion(bf16[640,256]{1,0:T(8,128)(2,1)S(1)} %copy-done, f32[32,256]{1,0:T(8,128)} %shard_map.17), kind=kOutput, calls=%fused_computation.3 | convolution fusion | flops 10514432 | bytes 401408 | tf_op jit(solution)/shard_map/dot_general | solution.py:145
  37.9 0.0 copy-done.1
  38.0 1.5 %convolution_convert_fusion = bf16[256,640]{1,0:T(8,128)(2,1)S(1)} fusion(bf16[32,640]{1,0:T(8,128)(2,1)S(1)} %convolution_convert_fusion.1, bf16[640,256]{1,0:T(8,128)(2,1)S(1)} %copy-done, s32[256]{0:T(256)S(1)} %iota_add_fusion, pred[256]{0:T(512)(128)(4,1)S(1)} %iota_compare_fusion, f32[32,256]{1,0:T(8,128)S(1)} %copy-done.1), kind=kOutput, calls=%fused_computation.1 | convolution fusion | flops 96215040 | bytes 730368 | tf_op jit(solution)/shard_map/dot_general | solution.py:150
  39.5 16.3 %all_to_all.5 = bf16[8,32,640]{2,1,0:T(8,128)(2,1)S(1)} all-to-all(bf16[8,32,640]{2,1,0:T(8,128)(2,1)S(1)} %bitcast.9), channel_id=1, replica_groups=mesh['groups'=2,'pix'=4,'sub'=2,'inner'=2] {'pix','sub'}, dimensions={0} | all-to-all | bytes 655360 | tf_op jit(solution)/shard_map/all_to_all | solution.py:155
  55.8 0.8 %copy.5 = bf16[32,8,640]{2,1,0:T(8,128)(2,1)} copy(bf16[32,8,640]{2,0,1:T(8,128)(2,1)S(1)} %bitcast.8) | data formatting | bytes 655360 | tf_op jit(solution)/shard_map/transpose | solution.py:156
  (10 shorter events, 0.1 us)
Async XLA Ops:
  1.4 1.5 %collective-permute-start = (f32[192,128]{1,0:T(8,128)S(1)}, f32[192,128]{1,0:T(8,128)S(1)}, u32[]{:S(2)}, u32[]{:S(2)}) collective-permute-start(f32[192,128]{1,0:T(8,128)S(1)} %slice_select_fusion), channel_id=1, source_target_pairs={{0,1},{1,0},{2,3},{3,2},{4,5},{5,4},{6,7},{7,6},{8,9},{9,8},{10,11... | collective-permute-start | bytes 294920 | tf_op jit(solution)/shard_map/ppermute | solution.py:77
  3.0 6.0 %collective-permute-start.1 = (f32[192,128]{1,0:T(8,128)S(1)}, f32[192,128]{1,0:T(8,128)S(1)}, u32[]{:S(2)}, u32[]{:S(2)}) collective-permute-start(f32[192,128]{1,0:T(8,128)S(1)} %select_add_fusion), channel_id=1, source_target_pairs={{0,2},{2,0},{1,3},{3,1},{4,6},{6,4},{5,7},{7,5},{8,10},{10,8},{9,1... | collective-permute-start | bytes 294920 | tf_op jit(solution)/shard_map/ppermute | solution.py:107
  5.9 5.5 %collective-permute-start.2 = (f32[192,128]{1,0:T(8,128)S(1)}, f32[192,128]{1,0:T(8,128)S(1)}, u32[]{:S(2)}, u32[]{:S(2)}) collective-permute-start(f32[192,128]{1,0:T(8,128)S(1)} %select_add_fusion), channel_id=1, source_target_pairs={{0,4},{4,0},{8,12},{12,8},{1,5},{5,1},{9,13},{13,9},{2,6},{6,2},{1... | collective-permute-start | bytes 294920 | tf_op jit(solution)/shard_map/ppermute | solution.py:108
  7.4 5.5 %collective-permute-start.3 = (f32[192,128]{1,0:T(8,128)S(1)}, f32[192,128]{1,0:T(8,128)S(1)}, u32[]{:S(2)}, u32[]{:S(2)}) collective-permute-start(f32[192,128]{1,0:T(8,128)S(1)} %select_add_fusion), channel_id=1, source_target_pairs={{0,6},{2,4},{4,2},{6,0},{8,14},{10,12},{12,10},{14,8},{1,7},{3,5},... | collective-permute-start | bytes 294920 | tf_op jit(solution)/shard_map/ppermute | solution.py:115
  13.0 6.6 %collective-permute-start.4 = (f32[192,128]{1,0:T(8,128)S(1)}, f32[192,128]{1,0:T(8,128)S(1)}, u32[]{:S(2)}, u32[]{:S(2)}) collective-permute-start(f32[192,128]{1,0:T(8,128)S(1)} %add_add_fusion), channel_id=1, source_target_pairs={{0,8},{4,12},{8,0},{12,4},{1,9},{5,13},{9,1},{13,5},{2,10},{6,14},... | collective-permute-start | bytes 294920 | tf_op jit(solution)/shard_map/ppermute | solution.py:129
  19.6 1.4 %collective-permute-start.5 = (f32[192,128]{1,0:T(8,128)S(1)}, f32[192,128]{1,0:T(8,128)S(1)}, u32[]{:S(2)}, u32[]{:S(2)}) collective-permute-start(f32[192,128]{1,0:T(8,128)S(1)} %add.34), channel_id=1, source_target_pairs={{0,1},{1,0},{2,3},{3,2},{4,5},{5,4},{6,7},{7,6},{8,9},{9,8},{10,11... | collective-permute-start | bytes 294920 | tf_op jit(solution)/shard_map/ppermute | solution.py:82
  21.1 15.8 %copy-start = (bf16[640,256]{1,0:T(8,128)(2,1)S(1)}, bf16[640,256]{1,0:T(8,128)(2,1)}, u32[]{:S(2)}) copy-start(bf16[640,256]{1,0:T(8,128)(2,1)} %param.1) | copy-start | bytes 983044
  36.9 1.0 %copy-start.1 = (f32[32,256]{1,0:T(8,128)S(1)}, f32[32,256]{1,0:T(8,128)}, u32[]{:S(2)}) copy-start(f32[32,256]{1,0:T(8,128)} %shard_map.17) | copy-start | bytes 98308

commit v6 on v5

--- a/solution.py
+++ b/solution.py
@@ -1,6 +1,8 @@
 import math
 
 import jax
+import ml_dtypes
+import numpy as np
 import jax.numpy as jnp
 from jax import lax
 from jax.experimental import pallas as pl
@@ -12,9 +14,9 @@
 HI = lax.Precision.HIGHEST
 
 
-def modes_kernel(g_ref, out_ref):
+def spectra_kernel(g_ref, cube_ref, table_ref, out_ref):
     g = g_ref[...]
-    m = out_ref.shape[0]
+    m = MODES
     rows = lax.broadcasted_iota(jnp.int32, (m, 1), 0)
     cols = lax.broadcasted_iota(jnp.int32, (1, m), 1)
     xt = g[:m, :]
@@ -30,27 +32,34 @@
             rrow = jnp.where(cols > j, c[j:j + 1, :] / d, 0.0)
             xt = jnp.where(rows == j, q, xt - rcol * q)
             c = c - rcol * rrow
-    out_ref[...] = xt
+    modes_t = xt.astype(jnp.bfloat16)
+    cube = cube_ref[...]
+    nt = (((1,), (1,)), ((), ()))
+    amplitudes = lax.dot_general(cube, modes_t, nt, preferred_element_type=jnp.float32)
+    foreground = jnp.dot(amplitudes.astype(jnp.bfloat16), modes_t, preferred_element_type=jnp.float32)
+    cleaned = (cube.astype(jnp.float32) - foreground).astype(jnp.bfloat16)
+    coefficients = lax.dot_general(table_ref[...], cleaned, nt, preferred_element_type=jnp.float32)
+    out_ref[...] = coefficients.astype(out_ref.dtype)
 
 
-def leading_modes_t(gram):
-    n = gram.shape[0]
+def spectra_of(gram, cube, table):
+    vmem = pl.BlockSpec(memory_space=pltpu.VMEM)
     return pl.pallas_call(
-        modes_kernel,
-        out_shape=jax.ShapeDtypeStruct((MODES, n), jnp.float32),
-        in_specs=[pl.BlockSpec(memory_space=pltpu.VMEM)],
-        out_specs=pl.BlockSpec(memory_space=pltpu.VMEM),
-    )(gram)
+        spectra_kernel,
+        out_shape=jax.ShapeDtypeStruct((table.shape[0], cube.shape[0]), jnp.bfloat16),
+        in_specs=[vmem, vmem, vmem],
+        out_specs=vmem,
+    )(gram, cube, table)
 
 
 def delay_table(channels):
     middle = channels // 2
-    row_index = lax.broadcasted_iota(jnp.int32, (channels, channels), 0)
-    col_index = lax.broadcasted_iota(jnp.int32, (channels, channels), 1)
-    harmonic = jnp.where(row_index <= middle, row_index, row_index - middle)
-    angles = (harmonic * col_index % channels).astype(jnp.float32) * (2.0 * math.pi / channels)
-    values = jnp.where(row_index <= middle, jnp.cos(angles), jnp.sin(angles)) / math.sqrt(channels)
-    return values.astype(jnp.bfloat16)
+    row_index = np.arange(channels, dtype=np.int32)[:, None]
+    col_index = np.arange(channels, dtype=np.int32)[None, :]
+    harmonic = np.where(row_index <= middle, row_index, row_index - middle)
+    angles = ((harmonic * col_index) % channels).astype(np.float32) * np.float32(2.0 * math.pi / channels)
+    values = np.where(row_index <= middle, np.cos(angles), np.sin(angles)) / np.float32(math.sqrt(channels))
+    return values.astype(np.float32).astype(ml_dtypes.bfloat16)
 
 
 def sym_pack(g):
@@ -141,15 +150,7 @@
             cube, cube, (((0,), (0,)), ((), ())), preferred_element_type=jnp.float32
         )
         gram_matrix = gram_sum(partial_gram, mesh) / pixel_count
-        modes_b = leading_modes_t(gram_matrix).T.astype(jnp.bfloat16)
-        amplitudes = jnp.dot(cube, modes_b, preferred_element_type=jnp.float32).astype(jnp.bfloat16)
-        cleaned = (cube - jnp.dot(amplitudes, modes_b.T, preferred_element_type=jnp.float32)).astype(
-            jnp.bfloat16
-        )
-        table_b = delay_table(channels)
-        coefficients = lax.dot_general(
-            table_b, cleaned, (((1,), (1,)), ((), ())), preferred_element_type=jnp.float32
-        ).astype(jnp.bfloat16)
+        coefficients = spectra_of(gram_matrix, cube, jnp.asarray(delay_table(channels)))
         k = lax.axis_size(("pix", "sub"))
         blocks = coefficients.reshape(k, coefficients.shape[0] // k, coefficients.shape[1])
         blocks = lax.all_to_all(blocks, ("pix", "sub"), split_axis=0, concat_axis=0, tiled=True)

time: 56.9 us -> 56 us (0.984)
  matrix products: 3.91 us -> 1.38 us
  Pallas kernels: 15 us -> 15.9 us
  blocking collectives: 16.3 us -> 17.2 us
    ppermute x1, starting transfers between devices: 0.01 us -> 3.91 us  [paired_round(): r12 = lax.ppermute(x, (a1, a2), pairs)]
    ppermute x1, starting transfers between devices: 2.89 us -> 0.19 us  [paired_round(): r1 = lax.ppermute(x, a1, xor_perm(n1, d1))]
    dot_general x2 -> x0, matrix products: 2.54 us -> none  [the longest x1 1.51 us: local(): lax.dot_general(table_b, cleaned, (((1,), (1,)), ((), ())), preferred_ele...]
    ppermute x1, waiting for transfers between devices: 1.53 us -> 0.01 us  [paired_round(): r1 = lax.ppermute(x, a1, xor_perm(n1, d1))]
    ppermute x1, waiting for transfers between devices: 1.6 us -> 3 us  [paired_round(): r12 = lax.ppermute(x, (a1, a2), pairs)]
    ppermute x1, starting transfers between devices: 1.58 us -> 0.45 us  [paired_round(): r2 = lax.ppermute(x, a2, xor_perm(n2, d2))]
    all_to_all x1, blocking collectives: 16.3 us -> 17.2 us  [local(): lax.all_to_all(blocks, ('pix', 'sub'), split_axis=0, concat_axis=0, tiled...]
    pallas_call x1, Pallas kernels: 15 us -> 15.9 us  [spectra_of(): pl.pallas_call(spectra_kernel, out_shape=jax.ShapeDtypeStruct((table.shap...]
  transfers between devices with their start and end apart: 6 -> 6, of which waited for: 6 -> 5; matrix products, arithmetic and copies ran while one was open for 0% -> 0% of each run, Pallas kernels for 0% -> 0%
where the time goes in v6:
time: 56 us; the launch traced here: 55.8 us
  blocking collectives  17.2 us (31%)
  Pallas kernels  15.9 us (28%)
  waiting for transfers between devices  11.5 us (21%)
  starting transfers between devices  7.9 us (14%)
  matrix products  1.38 us (2%)
  local copies, waits for them, and re-layouts  0.95 us (2%)
  other arithmetic  0.82 us (1%)
    all_to_all x1, blocking collectives, local(): lax.all_to_all(blocks, ('pix', 'sub'), split_axis=0, concat_axis=0, tiled...  17.2 us
    pallas_call x1, Pallas kernels, spectra_of(): pl.pallas_call(spectra_kernel, out_shape=jax.ShapeDtypeStruct((table.shap...  15.9 us
    ppermute x1, waiting for transfers between devices, gram_sum(): x = x + lax.ppermute(x, name, xor_perm(n, d))  4.5 us
    ppermute x1, starting transfers between devices, paired_round(): r12 = lax.ppermute(x, (a1, a2), pairs)  3.91 us
    ppermute x1, waiting for transfers between devices, paired_round(): r12 = lax.ppermute(x, (a1, a2), pairs)  3 us
    ppermute x1, starting transfers between devices, gram_sum(): x = x + lax.ppermute(x, name, xor_perm(n, d))  2.72 us
    ppermute x1, waiting for transfers between devices, paired_round(): r2 = lax.ppermute(x, a2, xor_perm(n2, d2))  1.74 us
    dot_general x1, matrix products, local(): lax.dot_general(cube, cube, (((0,), (0,)), ((), ())), preferred_element_t...  1.38 us
  transfers between devices with their start and end apart: 6, of which 5 were waited for; matrix products, arithmetic and copies ran while one was open for 0% of the time, Pallas kernels for 0%

profile of v6, /device:TPU:0, one launch (start us, length us, event | category | flops | bytes accessed | tf_op | source)
XLA Modules:
  0.0 55.8 jit_solution(10593689208672184685)
XLA Ops:
  0.0 1.4 %fusion.1 = f32[256,256]{1,0:T(8,128)S(1)} fusion(bf16[640,256]{1,0:T(8,128)(2,1)} %cube_ref.1), kind=kOutput, calls=%fused_computation.8 | convolution fusion | flops 83886080 | bytes 589824 | tf_op jit(solution)/shard_map/dot_general | solution.py:149
  1.5 0.6 %collective-permute-start = (f32[192,128]{1,0:T(8,128)S(1)}, f32[192,128]{1,0:T(8,128)S(1)}, u32[]{:S(2)}, u32[]{:S(2)}) collective-permute-start(f32[192,128]{1,0:T(8,128)S(1)} %slice_select_fusion), channel_id=1, source_target_pairs={{0,1},{1,0},{2,3},{3,2},{4,5},{5,4},{6,7},{7,6},{8,9},{9,8},{10,11... | collective-permute-start | bytes 294920 | tf_op jit(solution)/shard_map/ppermute | solution.py:86
  2.0 0.9 %collective-permute-done = f32[192,128]{1,0:T(8,128)S(1)} collective-permute-done((f32[192,128]{1,0:T(8,128)S(1)}, f32[192,128]{1,0:T(8,128)S(1)}, u32[]{:S(2)}, u32[]{:S(2)}) %collective-permute-start) | collective-permute-done | bytes 98336 | tf_op jit(solution)/shard_map/ppermute | solution.py:86
  3.0 3.9 %collective-permute-start.3 = (f32[192,128]{1,0:T(8,128)S(1)}, f32[192,128]{1,0:T(8,128)S(1)}, u32[]{:S(2)}, u32[]{:S(2)}) collective-permute-start(f32[192,128]{1,0:T(8,128)S(1)} %select_add_fusion), channel_id=1, source_target_pairs={{0,6},{2,4},{4,2},{6,0},{8,14},{10,12},{12,10},{14,8},{1,7},{3,5},... | collective-permute-start | bytes 294920 | tf_op jit(solution)/shard_map/ppermute | solution.py:124
  6.9 0.4 collective-permute-start.2
  7.3 0.2 collective-permute-start.1
  7.5 3.0 %collective-permute-done.3 = f32[192,128]{1,0:T(8,128)S(1)} collective-permute-done((f32[192,128]{1,0:T(8,128)S(1)}, f32[192,128]{1,0:T(8,128)S(1)}, u32[]{:S(2)}, u32[]{:S(2)}) %collective-permute-start.3) | collective-permute-done | bytes 98336 | tf_op jit(solution)/shard_map/ppermute | solution.py:124
  10.5 1.7 %collective-permute-done.2 = f32[192,128]{1,0:T(8,128)S(1)} collective-permute-done((f32[192,128]{1,0:T(8,128)S(1)}, f32[192,128]{1,0:T(8,128)S(1)}, u32[]{:S(2)}, u32[]{:S(2)}) %collective-permute-start.2) | collective-permute-done | bytes 98336 | tf_op jit(solution)/shard_map/ppermute | solution.py:117
  12.3 0.0 collective-permute-done.1
  12.3 2.7 %collective-permute-start.4 = (f32[192,128]{1,0:T(8,128)S(1)}, f32[192,128]{1,0:T(8,128)S(1)}, u32[]{:S(2)}, u32[]{:S(2)}) collective-permute-start(f32[192,128]{1,0:T(8,128)S(1)} %add_add_fusion), channel_id=1, source_target_pairs={{0,8},{4,12},{8,0},{12,4},{1,9},{5,13},{9,1},{13,5},{2,10},{6,14},... | collective-permute-start | bytes 294920 | tf_op jit(solution)/shard_map/ppermute | solution.py:138
  15.0 4.5 %collective-permute-done.4 = f32[192,128]{1,0:T(8,128)S(1)} collective-permute-done((f32[192,128]{1,0:T(8,128)S(1)}, f32[192,128]{1,0:T(8,128)S(1)}, u32[]{:S(2)}, u32[]{:S(2)}) %collective-permute-start.4) | collective-permute-done | bytes 98336 | tf_op jit(solution)/shard_map/ppermute | solution.py:138
  19.5 0.1 collective-permute-start.5
  19.6 1.3 %collective-permute-done.5 = f32[192,128]{1,0:T(8,128)S(1)} collective-permute-done((f32[192,128]{1,0:T(8,128)S(1)}, f32[192,128]{1,0:T(8,128)S(1)}, u32[]{:S(2)}, u32[]{:S(2)}) %collective-permute-start.5) | collective-permute-done | bytes 98336 | tf_op jit(solution)/shard_map/ppermute | solution.py:91
  21.0 0.1 copy.5
  21.1 0.7 %maximum_multiply_fusion.g_ref = f32[256,256]{1,0:T(8,128)} fusion(f32[128,128]{1,0:T(8,128)S(1)} %get-tuple-element.7, f32[128,128]{1,0:T(8,128)S(1)} %copy.5, f32[128,128]{1,0:T(8,128)S(1)} %get-tuple-element.8, f32[128,128]{1,0:T(8,128)S(1)} %get-tuple-element.5), kind=kLoop, calls=%fused_computation | loop fusion | flops 262144 | bytes 524288 | tf_op jit(solution)/shard_map/div | solution.py:152
  21.8 15.9 %shard_map.28 = bf16[256,640]{1,0:T(8,128)(2,1)} custom-call(f32[256,256]{1,0:T(8,128)} %maximum_multiply_fusion.g_ref, bf16[640,256]{1,0:T(8,128)(2,1)} %cube_ref.1, bf16[256,256]{1,0:T(8,128)(2,1)} %constant.38.clone.table_ref), custom_call_target="tpu_custom_call" | custom-call | tf_op jit(solution)/shard_map/pallas_call | solution.py:47
  37.7 17.2 %all_to_all.5 = bf16[8,32,640]{2,1,0:T(8,128)(2,1)S(1)} all-to-all(bf16[8,32,640]{2,1,0:T(8,128)(2,1)} %bitcast.6), channel_id=1, replica_groups=mesh['groups'=2,'pix'=4,'sub'=2,'inner'=2] {'pix','sub'}, dimensions={0} | all-to-all | bytes 655360 | tf_op jit(solution)/shard_map/all_to_all | solution.py:156
  54.9 0.8 %copy.6 = bf16[32,8,640]{2,1,0:T(8,128)(2,1)} copy(bf16[32,8,640]{2,0,1:T(8,128)(2,1)S(1)} %bitcast.7) | data formatting | bytes 655360 | tf_op jit(solution)/shard_map/transpose | solution.py:157
  (8 shorter events, 0.1 us)
Async XLA Ops:
  1.5 1.5 %collective-permute-start = (f32[192,128]{1,0:T(8,128)S(1)}, f32[192,128]{1,0:T(8,128)S(1)}, u32[]{:S(2)}, u32[]{:S(2)}) collective-permute-start(f32[192,128]{1,0:T(8,128)S(1)} %slice_select_fusion), channel_id=1, source_target_pairs={{0,1},{1,0},{2,3},{3,2},{4,5},{5,4},{6,7},{7,6},{8,9},{9,8},{10,11... | collective-permute-start | bytes 294920 | tf_op jit(solution)/shard_map/ppermute | solution.py:86
  3.0 7.6 %collective-permute-start.3 = (f32[192,128]{1,0:T(8,128)S(1)}, f32[192,128]{1,0:T(8,128)S(1)}, u32[]{:S(2)}, u32[]{:S(2)}) collective-permute-start(f32[192,128]{1,0:T(8,128)S(1)} %select_add_fusion), channel_id=1, source_target_pairs={{0,6},{2,4},{4,2},{6,0},{8,14},{10,12},{12,10},{14,8},{1,7},{3,5},... | collective-permute-start | bytes 294920 | tf_op jit(solution)/shard_map/ppermute | solution.py:124
  6.9 5.4 %collective-permute-start.2 = (f32[192,128]{1,0:T(8,128)S(1)}, f32[192,128]{1,0:T(8,128)S(1)}, u32[]{:S(2)}, u32[]{:S(2)}) collective-permute-start(f32[192,128]{1,0:T(8,128)S(1)} %select_add_fusion), channel_id=1, source_target_pairs={{0,4},{4,0},{8,12},{12,8},{1,5},{5,1},{9,13},{13,9},{2,6},{6,2},{1... | collective-permute-start | bytes 294920 | tf_op jit(solution)/shard_map/ppermute | solution.py:117
  7.3 4.9 %collective-permute-start.1 = (f32[192,128]{1,0:T(8,128)S(1)}, f32[192,128]{1,0:T(8,128)S(1)}, u32[]{:S(2)}, u32[]{:S(2)}) collective-permute-start(f32[192,128]{1,0:T(8,128)S(1)} %select_add_fusion), channel_id=1, source_target_pairs={{0,2},{2,0},{1,3},{3,1},{4,6},{6,4},{5,7},{7,5},{8,10},{10,8},{9,1... | collective-permute-start | bytes 294920 | tf_op jit(solution)/shard_map/ppermute | solution.py:116
  12.3 7.2 %collective-permute-start.4 = (f32[192,128]{1,0:T(8,128)S(1)}, f32[192,128]{1,0:T(8,128)S(1)}, u32[]{:S(2)}, u32[]{:S(2)}) collective-permute-start(f32[192,128]{1,0:T(8,128)S(1)} %add_add_fusion), channel_id=1, source_target_pairs={{0,8},{4,12},{8,0},{12,4},{1,9},{5,13},{9,1},{13,5},{2,10},{6,14},... | collective-permute-start | bytes 294920 | tf_op jit(solution)/shard_map/ppermute | solution.py:138
  19.5 1.4 %collective-permute-start.5 = (f32[192,128]{1,0:T(8,128)S(1)}, f32[192,128]{1,0:T(8,128)S(1)}, u32[]{:S(2)}, u32[]{:S(2)}) collective-permute-start(f32[192,128]{1,0:T(8,128)S(1)} %add.26), channel_id=1, source_target_pairs={{0,1},{1,0},{2,3},{3,2},{4,5},{5,4},{6,7},{7,6},{8,9},{9,8},{10,11... | collective-permute-start | bytes 294920 | tf_op jit(solution)/shard_map/ppermute | solution.py:91

commit v7 on v6

--- a/solution.py
+++ b/solution.py
@@ -63,14 +63,22 @@
 
 
 def sym_pack(g):
-    h = g.shape[0] // 2
-    return jnp.concatenate([g[:h, :h], g[:h, h:], g[h:, h:]], axis=0)
+    q = g.shape[0] // 4
+    blk = lambda i, j: g[i * q:(i + 1) * q, j * q:(j + 1) * q]
+    slabs = [g[0:q, 0:2 * q], g[0:q, 2 * q:4 * q], g[q:2 * q, q:3 * q],
+             jnp.concatenate([blk(1, 3), blk(3, 3)], axis=1), g[2 * q:3 * q, 2 * q:4 * q]]
+    return jnp.concatenate(slabs, axis=0)
 
 
 def sym_unpack(packed):
-    h = packed.shape[0] // 3
-    a, b, d = packed[:h], packed[h:2 * h], packed[2 * h:]
-    return jnp.concatenate([jnp.concatenate([a, b], 1), jnp.concatenate([b.T, d], 1)], 0)
+    q = packed.shape[1] // 2
+    s = [packed[k * q:(k + 1) * q] for k in range(5)]
+    b = {(0, 0): s[0][:, :q], (0, 1): s[0][:, q:], (0, 2): s[1][:, :q], (0, 3): s[1][:, q:],
+         (1, 1): s[2][:, :q], (1, 2): s[2][:, q:], (1, 3): s[3][:, :q], (3, 3): s[3][:, q:],
+         (2, 2): s[4][:, :q], (2, 3): s[4][:, q:]}
+    rows = [jnp.concatenate([b[(i, j)] if i <= j else b[(j, i)].T for j in range(4)], axis=1)
+            for i in range(4)]
+    return jnp.concatenate(rows, axis=0)
 
 
 def xor_perm(n, d):

time: 56 us -> 55.3 us (0.987)
  waiting for transfers between devices: 11.5 us -> 9.43 us
  local copies, waits for them, and re-layouts: 0.95 us -> 1.59 us
  blocking collectives: 17.2 us -> 17.8 us
    ppermute x1, waiting for transfers between devices: 4.5 us -> 3 us  [gram_sum(): x = x + lax.ppermute(x, name, xor_perm(n, d))]
    all_to_all x1, blocking collectives: 17.2 us -> 17.8 us  [local(): lax.all_to_all(blocks, ('pix', 'sub'), split_axis=0, concat_axis=0, tiled...]
  transfers between devices with their start and end apart: 6 -> 6, of which waited for: 5 -> 6; matrix products, arithmetic and copies ran while one was open for 0% -> 0% of each run, Pallas kernels for 0% -> 0%
where the time goes in v7:
time: 55.3 us; the launch traced here: 55 us
  blocking collectives  17.8 us (32%)
  Pallas kernels  15.9 us (29%)
  waiting for transfers between devices  9.43 us (17%)
  starting transfers between devices  7.76 us (14%)
  local copies, waits for them, and re-layouts  1.59 us (3%)
  matrix products  1.38 us (2%)
  other arithmetic  1.06 us (2%)
    all_to_all x1, blocking collectives, local(): lax.all_to_all(blocks, ('pix', 'sub'), split_axis=0, concat_axis=0, tiled...  17.8 us
    pallas_call x1, Pallas kernels, spectra_of(): pl.pallas_call(spectra_kernel, out_shape=jax.ShapeDtypeStruct((table.shap...  15.9 us
    ppermute x1, starting transfers between devices, paired_round(): r12 = lax.ppermute(x, (a1, a2), pairs)  3.89 us
    ppermute x1, waiting for transfers between devices, gram_sum(): x = x + lax.ppermute(x, name, xor_perm(n, d))  3 us
    ppermute x1, starting transfers between devices, gram_sum(): x = x + lax.ppermute(x, name, xor_perm(n, d))  2.65 us
    ppermute x1, waiting for transfers between devices, paired_round(): r12 = lax.ppermute(x, (a1, a2), pairs)  2.44 us
    ppermute x1, waiting for transfers between devices, paired_round(): r2 = lax.ppermute(x, a2, xor_perm(n2, d2))  1.59 us
    dot_general x1, matrix products, local(): lax.dot_general(cube, cube, (((0,), (0,)), ((), ())), preferred_element_t...  1.38 us
  transfers between devices with their start and end apart: 6, of which 6 were waited for; matrix products, arithmetic and copies ran while one was open for 0% of the time, Pallas kernels for 0%

profile of v7, /device:TPU:0, one launch (start us, length us, event | category | flops | bytes accessed | tf_op | source)
XLA Modules:
  0.0 55.0 jit_solution(17989305341324007712)
XLA Ops:
  0.0 1.4 %fusion.5 = f32[256,256]{1,0:T(8,128)S(1)} fusion(bf16[640,256]{1,0:T(8,128)(2,1)} %cube_ref.1), kind=kOutput, calls=%fused_computation.17 | convolution fusion | flops 83886080 | bytes 589824 | tf_op jit(solution)/shard_map/dot_general | solution.py:157
  1.4 0.1 fusion.1
  1.5 0.1 fusion.2
  1.6 0.1 fusion
  1.6 0.5 collective-permute-start
  2.1 0.9 %collective-permute-done = f32[160,128]{1,0:T(8,128)S(1)} collective-permute-done((f32[160,128]{1,0:T(8,128)S(1)}, f32[160,128]{1,0:T(8,128)S(1)}, u32[]{:S(2)}, u32[]{:S(2)}) %collective-permute-start) | collective-permute-done | bytes 81952 | tf_op jit(solution)/shard_map/ppermute | solution.py:94
  3.1 0.1 select_add_fusion
  3.2 3.9 %collective-permute-start.3 = (f32[160,128]{1,0:T(8,128)S(1)}, f32[160,128]{1,0:T(8,128)S(1)}, u32[]{:S(2)}, u32[]{:S(2)}) collective-permute-start(f32[160,128]{1,0:T(8,128)S(1)} %select_add_fusion), channel_id=1, source_target_pairs={{0,6},{2,4},{4,2},{6,0},{8,14},{10,12},{12,10},{14,8},{1,7},{3,5},... | collective-permute-start | bytes 245768 | tf_op jit(solution)/shard_map/ppermute | solution.py:132
  7.0 0.4 collective-permute-start.2
  7.5 0.2 collective-permute-start.1
  7.7 2.4 %collective-permute-done.3 = f32[160,128]{1,0:T(8,128)S(1)} collective-permute-done((f32[160,128]{1,0:T(8,128)S(1)}, f32[160,128]{1,0:T(8,128)S(1)}, u32[]{:S(2)}, u32[]{:S(2)}) %collective-permute-start.3) | collective-permute-done | bytes 81952 | tf_op jit(solution)/shard_map/ppermute | solution.py:132
  10.1 1.6 %collective-permute-done.2 = f32[160,128]{1,0:T(8,128)S(1)} collective-permute-done((f32[160,128]{1,0:T(8,128)S(1)}, f32[160,128]{1,0:T(8,128)S(1)}, u32[]{:S(2)}, u32[]{:S(2)}) %collective-permute-start.2) | collective-permute-done | bytes 81952 | tf_op jit(solution)/shard_map/ppermute | solution.py:125
  11.7 0.2 collective-permute-done.1
  12.0 2.7 %collective-permute-start.4 = (f32[160,128]{1,0:T(8,128)S(1)}, f32[160,128]{1,0:T(8,128)S(1)}, u32[]{:S(2)}, u32[]{:S(2)}) collective-permute-start(f32[160,128]{1,0:T(8,128)S(1)} %add_add_fusion), channel_id=1, source_target_pairs={{0,8},{4,12},{8,0},{12,4},{1,9},{5,13},{9,1},{13,5},{2,10},{6,14},... | collective-permute-start | bytes 245768 | tf_op jit(solution)/shard_map/ppermute | solution.py:146
  14.6 3.0 %collective-permute-done.4 = f32[160,128]{1,0:T(8,128)S(1)} collective-permute-done((f32[160,128]{1,0:T(8,128)S(1)}, f32[160,128]{1,0:T(8,128)S(1)}, u32[]{:S(2)}, u32[]{:S(2)}) %collective-permute-start.4) | collective-permute-done | bytes 81952 | tf_op jit(solution)/shard_map/ppermute | solution.py:146
  17.6 0.1 collective-permute-start.5
  17.7 1.3 %collective-permute-done.5 = f32[160,128]{1,0:T(8,128)S(1)} collective-permute-done((f32[160,128]{1,0:T(8,128)S(1)}, f32[160,128]{1,0:T(8,128)S(1)}, u32[]{:S(2)}, u32[]{:S(2)}) %collective-permute-start.5) | collective-permute-done | bytes 81952 | tf_op jit(solution)/shard_map/ppermute | solution.py:99
  19.0 0.1 fusion.4
  19.1 0.1 copy.17
  19.2 0.1 copy.14
  19.3 0.1 copy.18
  19.3 0.1 copy.13
  19.4 0.1 copy.15
  19.5 0.1 copy.19
  19.6 0.9 %maximum_multiply_fusion.g_ref = f32[256,256]{1,0:T(8,128)} fusion(f32[64,64]{1,0:T(8,128)S(1)} %get-tuple-element.20, f32[64,64]{1,0:T(8,128)S(1)} %copy.15, f32[64,64]{1,0:T(8,128)S(1)} %copy.14, f32[64,64]{1,0:T(8,128)S(1)} %copy.13, f32[64,128]{1,0:T(8,128)S(1)} %get-tuple-element.12, f32[64,64]{1,0:T(8,128)S(1)} %bitcast.17, f32[64,64]{1,0:T(8,128)S(1)} %bitcast.16, ...), kind=kLoop, calls=%fused_computation | loop fusion | flops 786432 | bytes 524288 | tf_op jit(solution)/shard_map/div | solution.py:160
  20.5 15.9 %shard_map.28 = bf16[256,640]{1,0:T(8,128)(2,1)} custom-call(f32[256,256]{1,0:T(8,128)} %maximum_multiply_fusion.g_ref, bf16[640,256]{1,0:T(8,128)(2,1)} %cube_ref.1, bf16[256,256]{1,0:T(8,128)(2,1)} %constant.38.clone.table_ref), custom_call_target="tpu_custom_call" | custom-call | tf_op jit(solution)/shard_map/pallas_call | solution.py:47
  36.4 17.8 %all_to_all.5 = bf16[8,32,640]{2,1,0:T(8,128)(2,1)S(1)} all-to-all(bf16[8,32,640]{2,1,0:T(8,128)(2,1)} %bitcast.13), channel_id=1, replica_groups=mesh['groups'=2,'pix'=4,'sub'=2,'inner'=2] {'pix','sub'}, dimensions={0} | all-to-all | bytes 655360 | tf_op jit(solution)/shard_map/all_to_all | solution.py:164
  54.2 0.8 %copy.16 = bf16[32,8,640]{2,1,0:T(8,128)(2,1)} copy(bf16[32,8,640]{2,0,1:T(8,128)(2,1)S(1)} %bitcast.14) | data formatting | bytes 655360 | tf_op jit(solution)/shard_map/transpose | solution.py:165
  (4 shorter events, 0.1 us)
Async XLA Ops:
  1.6 1.4 %collective-permute-start = (f32[160,128]{1,0:T(8,128)S(1)}, f32[160,128]{1,0:T(8,128)S(1)}, u32[]{:S(2)}, u32[]{:S(2)}) collective-permute-start(f32[160,128]{1,0:T(8,128)S(1)} %fusion), channel_id=1, source_target_pairs={{0,1},{1,0},{2,3},{3,2},{4,5},{5,4},{6,7},{7,6},{8,9},{9,8},{10,11... | collective-permute-start | bytes 245768 | tf_op jit(solution)/shard_map/ppermute | solution.py:94
  3.2 7.0 %collective-permute-start.3 = (f32[160,128]{1,0:T(8,128)S(1)}, f32[160,128]{1,0:T(8,128)S(1)}, u32[]{:S(2)}, u32[]{:S(2)}) collective-permute-start(f32[160,128]{1,0:T(8,128)S(1)} %select_add_fusion), channel_id=1, source_target_pairs={{0,6},{2,4},{4,2},{6,0},{8,14},{10,12},{12,10},{14,8},{1,7},{3,5},... | collective-permute-start | bytes 245768 | tf_op jit(solution)/shard_map/ppermute | solution.py:132
  7.0 4.7 %collective-permute-start.2 = (f32[160,128]{1,0:T(8,128)S(1)}, f32[160,128]{1,0:T(8,128)S(1)}, u32[]{:S(2)}, u32[]{:S(2)}) collective-permute-start(f32[160,128]{1,0:T(8,128)S(1)} %select_add_fusion), channel_id=1, source_target_pairs={{0,4},{4,0},{8,12},{12,8},{1,5},{5,1},{9,13},{13,9},{2,6},{6,2},{1... | collective-permute-start | bytes 245768 | tf_op jit(solution)/shard_map/ppermute | solution.py:125
  7.5 4.4 %collective-permute-start.1 = (f32[160,128]{1,0:T(8,128)S(1)}, f32[160,128]{1,0:T(8,128)S(1)}, u32[]{:S(2)}, u32[]{:S(2)}) collective-permute-start(f32[160,128]{1,0:T(8,128)S(1)} %select_add_fusion), channel_id=1, source_target_pairs={{0,2},{2,0},{1,3},{3,1},{4,6},{6,4},{5,7},{7,5},{8,10},{10,8},{9,1... | collective-permute-start | bytes 245768 | tf_op jit(solution)/shard_map/ppermute | solution.py:124
  12.0 5.7 %collective-permute-start.4 = (f32[160,128]{1,0:T(8,128)S(1)}, f32[160,128]{1,0:T(8,128)S(1)}, u32[]{:S(2)}, u32[]{:S(2)}) collective-permute-start(f32[160,128]{1,0:T(8,128)S(1)} %add_add_fusion), channel_id=1, source_target_pairs={{0,8},{4,12},{8,0},{12,4},{1,9},{5,13},{9,1},{13,5},{2,10},{6,14},... | collective-permute-start | bytes 245768 | tf_op jit(solution)/shard_map/ppermute | solution.py:146
  17.6 1.3 %collective-permute-start.5 = (f32[160,128]{1,0:T(8,128)S(1)}, f32[160,128]{1,0:T(8,128)S(1)}, u32[]{:S(2)}, u32[]{:S(2)}) collective-permute-start(f32[160,128]{1,0:T(8,128)S(1)} %add.26), channel_id=1, source_target_pairs={{0,1},{1,0},{2,3},{3,2},{4,5},{5,4},{6,7},{7,6},{8,9},{9,8},{10,11... | collective-permute-start | bytes 245768 | tf_op jit(solution)/shard_map/ppermute | solution.py:99

commit v8 on v7

--- a/solution.py
+++ b/solution.py
@@ -64,21 +64,19 @@
 
 def sym_pack(g):
     q = g.shape[0] // 4
-    blk = lambda i, j: g[i * q:(i + 1) * q, j * q:(j + 1) * q]
-    slabs = [g[0:q, 0:2 * q], g[0:q, 2 * q:4 * q], g[q:2 * q, q:3 * q],
-             jnp.concatenate([blk(1, 3), blk(3, 3)], axis=1), g[2 * q:3 * q, 2 * q:4 * q]]
+    slabs = [g[0:q, 0:2 * q], g[0:q, 2 * q:4 * q], g[q:2 * q, 2 * q:4 * q],
+             jnp.concatenate([g[q:2 * q, q:2 * q], g[3 * q:4 * q, 3 * q:4 * q]], axis=1),
+             g[2 * q:3 * q, 2 * q:4 * q]]
     return jnp.concatenate(slabs, axis=0)
 
 
 def sym_unpack(packed):
     q = packed.shape[1] // 2
     s = [packed[k * q:(k + 1) * q] for k in range(5)]
-    b = {(0, 0): s[0][:, :q], (0, 1): s[0][:, q:], (0, 2): s[1][:, :q], (0, 3): s[1][:, q:],
-         (1, 1): s[2][:, :q], (1, 2): s[2][:, q:], (1, 3): s[3][:, :q], (3, 3): s[3][:, q:],
-         (2, 2): s[4][:, :q], (2, 3): s[4][:, q:]}
-    rows = [jnp.concatenate([b[(i, j)] if i <= j else b[(j, i)].T for j in range(4)], axis=1)
-            for i in range(4)]
-    return jnp.concatenate(rows, axis=0)
+    a = jnp.concatenate([s[0], jnp.concatenate([s[0][:, q:].T, s[3][:, :q]], axis=1)], axis=0)
+    d = jnp.concatenate([s[4], jnp.concatenate([s[4][:, q:].T, s[3][:, q:]], axis=1)], axis=0)
+    b = jnp.concatenate([s[1], s[2]], axis=0)
+    return jnp.concatenate([jnp.concatenate([a, b], axis=1), jnp.concatenate([b.T, d], axis=1)], axis=0)
 
 
 def xor_perm(n, d):

time: 55.3 us -> 55 us (level)
  no operation moved by 1% of the time
where the time goes in v8:
time: 55 us; the launch traced here: 54.7 us
  blocking collectives  17.8 us (32%)
  Pallas kernels  15.9 us (29%)
  waiting for transfers between devices  9.43 us (17%)
  starting transfers between devices  7.76 us (14%)
  matrix products  1.38 us (3%)
  local copies, waits for them, and re-layouts  1.28 us (2%)
  other arithmetic  1.03 us (2%)
    all_to_all x1, blocking collectives, local(): lax.all_to_all(blocks, ('pix', 'sub'), split_axis=0, concat_axis=0, tiled...  17.8 us
    pallas_call x1, Pallas kernels, spectra_of(): pl.pallas_call(spectra_kernel, out_shape=jax.ShapeDtypeStruct((table.shap...  15.9 us
    ppermute x1, starting transfers between devices, paired_round(): r12 = lax.ppermute(x, (a1, a2), pairs)  3.89 us
    ppermute x1, waiting for transfers between devices, gram_sum(): x = x + lax.ppermute(x, name, xor_perm(n, d))  3 us
    ppermute x1, starting transfers between devices, gram_sum(): x = x + lax.ppermute(x, name, xor_perm(n, d))  2.65 us
    ppermute x1, waiting for transfers between devices, paired_round(): r12 = lax.ppermute(x, (a1, a2), pairs)  2.44 us
    ppermute x1, waiting for transfers between devices, paired_round(): r2 = lax.ppermute(x, a2, xor_perm(n2, d2))  1.59 us
    dot_general x1, matrix products, local(): lax.dot_general(cube, cube, (((0,), (0,)), ((), ())), preferred_element_t...  1.38 us
  transfers between devices with their start and end apart: 6, of which 6 were waited for; matrix products, arithmetic and copies ran while one was open for 0% of the time, Pallas kernels for 0%

profile of v8, /device:TPU:0, one launch (start us, length us, event | category | flops | bytes accessed | tf_op | source)
XLA Modules:
  0.0 54.7 jit_solution(16613491222247174075)
XLA Ops:
  0.0 1.4 %fusion.6 = f32[256,256]{1,0:T(8,128)S(1)} fusion(bf16[640,256]{1,0:T(8,128)(2,1)} %cube_ref.1), kind=kOutput, calls=%fused_computation.16 | convolution fusion | flops 83886080 | bytes 589824 | tf_op jit(solution)/shard_map/dot_general | solution.py:155
  1.4 0.1 fusion.1
  1.5 0.1 fusion
  1.6 0.5 collective-permute-start
  2.1 0.9 %collective-permute-done = f32[160,128]{1,0:T(8,128)S(1)} collective-permute-done((f32[160,128]{1,0:T(8,128)S(1)}, f32[160,128]{1,0:T(8,128)S(1)}, u32[]{:S(2)}, u32[]{:S(2)}) %collective-permute-start) | collective-permute-done | bytes 81952 | tf_op jit(solution)/shard_map/ppermute | solution.py:92
  3.0 0.1 select_add_fusion
  3.1 3.9 %collective-permute-start.3 = (f32[160,128]{1,0:T(8,128)S(1)}, f32[160,128]{1,0:T(8,128)S(1)}, u32[]{:S(2)}, u32[]{:S(2)}) collective-permute-start(f32[160,128]{1,0:T(8,128)S(1)} %select_add_fusion), channel_id=1, source_target_pairs={{0,6},{2,4},{4,2},{6,0},{8,14},{10,12},{12,10},{14,8},{1,7},{3,5},... | collective-permute-start | bytes 245768 | tf_op jit(solution)/shard_map/ppermute | solution.py:130
  7.0 0.4 collective-permute-start.2
  7.4 0.2 collective-permute-start.1
  7.6 2.4 %collective-permute-done.3 = f32[160,128]{1,0:T(8,128)S(1)} collective-permute-done((f32[160,128]{1,0:T(8,128)S(1)}, f32[160,128]{1,0:T(8,128)S(1)}, u32[]{:S(2)}, u32[]{:S(2)}) %collective-permute-start.3) | collective-permute-done | bytes 81952 | tf_op jit(solution)/shard_map/ppermute | solution.py:130
  10.1 1.6 %collective-permute-done.2 = f32[160,128]{1,0:T(8,128)S(1)} collective-permute-done((f32[160,128]{1,0:T(8,128)S(1)}, f32[160,128]{1,0:T(8,128)S(1)}, u32[]{:S(2)}, u32[]{:S(2)}) %collective-permute-start.2) | collective-permute-done | bytes 81952 | tf_op jit(solution)/shard_map/ppermute | solution.py:123
  11.7 0.2 collective-permute-done.1
  11.9 2.7 %collective-permute-start.4 = (f32[160,128]{1,0:T(8,128)S(1)}, f32[160,128]{1,0:T(8,128)S(1)}, u32[]{:S(2)}, u32[]{:S(2)}) collective-permute-start(f32[160,128]{1,0:T(8,128)S(1)} %add_add_fusion), channel_id=1, source_target_pairs={{0,8},{4,12},{8,0},{12,4},{1,9},{5,13},{9,1},{13,5},{2,10},{6,14},... | collective-permute-start | bytes 245768 | tf_op jit(solution)/shard_map/ppermute | solution.py:144
  14.6 3.0 %collective-permute-done.4 = f32[160,128]{1,0:T(8,128)S(1)} collective-permute-done((f32[160,128]{1,0:T(8,128)S(1)}, f32[160,128]{1,0:T(8,128)S(1)}, u32[]{:S(2)}, u32[]{:S(2)}) %collective-permute-start.4) | collective-permute-done | bytes 81952 | tf_op jit(solution)/shard_map/ppermute | solution.py:144
  17.6 0.1 collective-permute-start.5
  17.7 1.3 %collective-permute-done.5 = f32[160,128]{1,0:T(8,128)S(1)} collective-permute-done((f32[160,128]{1,0:T(8,128)S(1)}, f32[160,128]{1,0:T(8,128)S(1)}, u32[]{:S(2)}, u32[]{:S(2)}) %collective-permute-start.5) | collective-permute-done | bytes 81952 | tf_op jit(solution)/shard_map/ppermute | solution.py:97
  19.0 0.1 fusion.4
  19.1 0.1 copy.11
  19.1 0.1 copy.8
  19.2 0.1 copy.9
  19.3 0.8 %maximum_multiply_fusion.g_ref = f32[256,256]{1,0:T(8,128)} fusion(f32[64,64]{1,0:T(8,128)S(1)} %get-tuple-element.12, f32[64,64]{1,0:T(8,128)S(1)} %copy.8, f32[64,128]{1,0:T(8,128)S(1)} %get-tuple-element.10, f32[128,128]{1,0:T(8,128)S(1)} %copy.9, f32[128,128]{1,0:T(8,128)S(1)} %get-tuple-element.15, f32[64,64]{1,0:T(8,128)S(1)} %get-tuple-element.14, ...), kind=kLoop, calls=%fused_computation | loop fusion | flops 524288 | bytes 524288 | tf_op jit(solution)/shard_map/div | solution.py:158
  20.1 15.9 %shard_map.28 = bf16[256,640]{1,0:T(8,128)(2,1)} custom-call(f32[256,256]{1,0:T(8,128)} %maximum_multiply_fusion.g_ref, bf16[640,256]{1,0:T(8,128)(2,1)} %cube_ref.1, bf16[256,256]{1,0:T(8,128)(2,1)} %constant.38.clone.table_ref), custom_call_target="tpu_custom_call" | custom-call | tf_op jit(solution)/shard_map/pallas_call | solution.py:47
  36.0 17.8 %all_to_all.5 = bf16[8,32,640]{2,1,0:T(8,128)(2,1)S(1)} all-to-all(bf16[8,32,640]{2,1,0:T(8,128)(2,1)} %bitcast.9), channel_id=1, replica_groups=mesh['groups'=2,'pix'=4,'sub'=2,'inner'=2] {'pix','sub'}, dimensions={0} | all-to-all | bytes 655360 | tf_op jit(solution)/shard_map/all_to_all | solution.py:162
  53.9 0.8 %copy.10 = bf16[32,8,640]{2,1,0:T(8,128)(2,1)} copy(bf16[32,8,640]{2,0,1:T(8,128)(2,1)S(1)} %bitcast.10) | data formatting | bytes 655360 | tf_op jit(solution)/shard_map/transpose | solution.py:163
  (7 shorter events, 0.1 us)
Async XLA Ops:
  1.6 1.4 %collective-permute-start = (f32[160,128]{1,0:T(8,128)S(1)}, f32[160,128]{1,0:T(8,128)S(1)}, u32[]{:S(2)}, u32[]{:S(2)}) collective-permute-start(f32[160,128]{1,0:T(8,128)S(1)} %fusion), channel_id=1, source_target_pairs={{0,1},{1,0},{2,3},{3,2},{4,5},{5,4},{6,7},{7,6},{8,9},{9,8},{10,11... | collective-permute-start | bytes 245768 | tf_op jit(solution)/shard_map/ppermute | solution.py:92
  3.1 7.0 %collective-permute-start.3 = (f32[160,128]{1,0:T(8,128)S(1)}, f32[160,128]{1,0:T(8,128)S(1)}, u32[]{:S(2)}, u32[]{:S(2)}) collective-permute-start(f32[160,128]{1,0:T(8,128)S(1)} %select_add_fusion), channel_id=1, source_target_pairs={{0,6},{2,4},{4,2},{6,0},{8,14},{10,12},{12,10},{14,8},{1,7},{3,5},... | collective-permute-start | bytes 245768 | tf_op jit(solution)/shard_map/ppermute | solution.py:130
  7.0 4.7 %collective-permute-start.2 = (f32[160,128]{1,0:T(8,128)S(1)}, f32[160,128]{1,0:T(8,128)S(1)}, u32[]{:S(2)}, u32[]{:S(2)}) collective-permute-start(f32[160,128]{1,0:T(8,128)S(1)} %select_add_fusion), channel_id=1, source_target_pairs={{0,4},{4,0},{8,12},{12,8},{1,5},{5,1},{9,13},{13,9},{2,6},{6,2},{1... | collective-permute-start | bytes 245768 | tf_op jit(solution)/shard_map/ppermute | solution.py:123
  7.4 4.4 %collective-permute-start.1 = (f32[160,128]{1,0:T(8,128)S(1)}, f32[160,128]{1,0:T(8,128)S(1)}, u32[]{:S(2)}, u32[]{:S(2)}) collective-permute-start(f32[160,128]{1,0:T(8,128)S(1)} %select_add_fusion), channel_id=1, source_target_pairs={{0,2},{2,0},{1,3},{3,1},{4,6},{6,4},{5,7},{7,5},{8,10},{10,8},{9,1... | collective-permute-start | bytes 245768 | tf_op jit(solution)/shard_map/ppermute | solution.py:122
  11.9 5.7 %collective-permute-start.4 = (f32[160,128]{1,0:T(8,128)S(1)}, f32[160,128]{1,0:T(8,128)S(1)}, u32[]{:S(2)}, u32[]{:S(2)}) collective-permute-start(f32[160,128]{1,0:T(8,128)S(1)} %add_add_fusion), channel_id=1, source_target_pairs={{0,8},{4,12},{8,0},{12,4},{1,9},{5,13},{9,1},{13,5},{2,10},{6,14},... | collective-permute-start | bytes 245768 | tf_op jit(solution)/shard_map/ppermute | solution.py:144
  17.6 1.3 %collective-permute-start.5 = (f32[160,128]{1,0:T(8,128)S(1)}, f32[160,128]{1,0:T(8,128)S(1)}, u32[]{:S(2)}, u32[]{:S(2)}) collective-permute-start(f32[160,128]{1,0:T(8,128)S(1)} %add.26), channel_id=1, source_target_pairs={{0,1},{1,0},{2,3},{3,2},{4,5},{5,4},{6,7},{7,6},{8,9},{9,8},{10,11... | collective-permute-start | bytes 245768 | tf_op jit(solution)/shard_map/ppermute | solution.py:97

commit v9 on v8

--- a/solution.py
+++ b/solution.py
@@ -14,7 +14,11 @@
 HI = lax.Precision.HIGHEST
 
 
-def spectra_kernel(g_ref, cube_ref, table_ref, out_ref):
+def spectra_kernel(g_ref, cube_hbm, table_hbm, out_ref, cube_ref, table_ref, sems):
+    cube_copy = pltpu.make_async_copy(cube_hbm, cube_ref, sems.at[0])
+    table_copy = pltpu.make_async_copy(table_hbm, table_ref, sems.at[1])
+    cube_copy.start()
+    table_copy.start()
     g = g_ref[...]
     m = MODES
     rows = lax.broadcasted_iota(jnp.int32, (m, 1), 0)
@@ -33,6 +37,8 @@
             xt = jnp.where(rows == j, q, xt - rcol * q)
             c = c - rcol * rrow
     modes_t = xt.astype(jnp.bfloat16)
+    cube_copy.wait()
+    table_copy.wait()
     cube = cube_ref[...]
     nt = (((1,), (1,)), ((), ()))
     amplitudes = lax.dot_general(cube, modes_t, nt, preferred_element_type=jnp.float32)
@@ -47,8 +53,10 @@
     return pl.pallas_call(
         spectra_kernel,
         out_shape=jax.ShapeDtypeStruct((table.shape[0], cube.shape[0]), jnp.bfloat16),
-        in_specs=[vmem, vmem, vmem],
+        in_specs=[vmem, pl.BlockSpec(memory_space=pl.ANY), pl.BlockSpec(memory_space=pl.ANY)],
         out_specs=vmem,
+        scratch_shapes=[pltpu.VMEM(cube.shape, cube.dtype), pltpu.VMEM(table.shape, table.dtype),
+                        pltpu.SemaphoreType.DMA((2,))],
     )(gram, cube, table)
 
 

time: 55 us -> 54.9 us (level)
  no operation moved by 1% of the time
where the time goes in v9:
time: 54.9 us; the launch traced here: 54.6 us
  blocking collectives  17.8 us (32%)
  Pallas kernels  15.8 us (29%)
  waiting for transfers between devices  9.43 us (17%)
  starting transfers between devices  7.76 us (14%)
  matrix products  1.38 us (3%)
  local copies, waits for them, and re-layouts  1.28 us (2%)
  other arithmetic  1.03 us (2%)
    all_to_all x1, blocking collectives, local(): lax.all_to_all(blocks, ('pix', 'sub'), split_axis=0, concat_axis=0, tiled...  17.8 us
    pallas_call x1, Pallas kernels, spectra_of(): pl.pallas_call(spectra_kernel, out_shape=jax.ShapeDtypeStruct((table.shap...  15.8 us
    ppermute x1, starting transfers between devices, paired_round(): r12 = lax.ppermute(x, (a1, a2), pairs)  3.89 us
    ppermute x1, waiting for transfers between devices, gram_sum(): x = x + lax.ppermute(x, name, xor_perm(n, d))  3 us
    ppermute x1, starting transfers between devices, gram_sum(): x = x + lax.ppermute(x, name, xor_perm(n, d))  2.65 us
    ppermute x1, waiting for transfers between devices, paired_round(): r12 = lax.ppermute(x, (a1, a2), pairs)  2.44 us
    ppermute x1, waiting for transfers between devices, paired_round(): r2 = lax.ppermute(x, a2, xor_perm(n2, d2))  1.59 us
    dot_general x1, matrix products, local(): lax.dot_general(cube, cube, (((0,), (0,)), ((), ())), preferred_element_t...  1.38 us
  transfers between devices with their start and end apart: 6, of which 6 were waited for; matrix products, arithmetic and copies ran while one was open for 0% of the time, Pallas kernels for 0%

profile of v9, /device:TPU:0, one launch (start us, length us, event | category | flops | bytes accessed | tf_op | source)
XLA Modules:
  0.0 54.6 jit_solution(5486903213999223313)
XLA Ops:
  0.0 1.4 %fusion.6 = f32[256,256]{1,0:T(8,128)S(1)} fusion(bf16[640,256]{1,0:T(8,128)(2,1)} %cube_hbm.1), kind=kOutput, calls=%fused_computation.16 | convolution fusion | flops 83886080 | bytes 589824 | tf_op jit(solution)/shard_map/dot_general | solution.py:163
  1.4 0.1 fusion.1
  1.5 0.1 fusion
  1.6 0.5 collective-permute-start
  2.1 0.9 %collective-permute-done = f32[160,128]{1,0:T(8,128)S(1)} collective-permute-done((f32[160,128]{1,0:T(8,128)S(1)}, f32[160,128]{1,0:T(8,128)S(1)}, u32[]{:S(2)}, u32[]{:S(2)}) %collective-permute-start) | collective-permute-done | bytes 81952 | tf_op jit(solution)/shard_map/ppermute | solution.py:100
  3.0 0.1 select_add_fusion
  3.1 3.9 %collective-permute-start.3 = (f32[160,128]{1,0:T(8,128)S(1)}, f32[160,128]{1,0:T(8,128)S(1)}, u32[]{:S(2)}, u32[]{:S(2)}) collective-permute-start(f32[160,128]{1,0:T(8,128)S(1)} %select_add_fusion), channel_id=1, source_target_pairs={{0,6},{2,4},{4,2},{6,0},{8,14},{10,12},{12,10},{14,8},{1,7},{3,5},... | collective-permute-start | bytes 245768 | tf_op jit(solution)/shard_map/ppermute | solution.py:138
  7.0 0.4 collective-permute-start.2
  7.4 0.2 collective-permute-start.1
  7.6 2.4 %collective-permute-done.3 = f32[160,128]{1,0:T(8,128)S(1)} collective-permute-done((f32[160,128]{1,0:T(8,128)S(1)}, f32[160,128]{1,0:T(8,128)S(1)}, u32[]{:S(2)}, u32[]{:S(2)}) %collective-permute-start.3) | collective-permute-done | bytes 81952 | tf_op jit(solution)/shard_map/ppermute | solution.py:138
  10.1 1.6 %collective-permute-done.2 = f32[160,128]{1,0:T(8,128)S(1)} collective-permute-done((f32[160,128]{1,0:T(8,128)S(1)}, f32[160,128]{1,0:T(8,128)S(1)}, u32[]{:S(2)}, u32[]{:S(2)}) %collective-permute-start.2) | collective-permute-done | bytes 81952 | tf_op jit(solution)/shard_map/ppermute | solution.py:131
  11.7 0.2 collective-permute-done.1
  11.9 2.7 %collective-permute-start.4 = (f32[160,128]{1,0:T(8,128)S(1)}, f32[160,128]{1,0:T(8,128)S(1)}, u32[]{:S(2)}, u32[]{:S(2)}) collective-permute-start(f32[160,128]{1,0:T(8,128)S(1)} %add_add_fusion), channel_id=1, source_target_pairs={{0,8},{4,12},{8,0},{12,4},{1,9},{5,13},{9,1},{13,5},{2,10},{6,14},... | collective-permute-start | bytes 245768 | tf_op jit(solution)/shard_map/ppermute | solution.py:152
  14.6 3.0 %collective-permute-done.4 = f32[160,128]{1,0:T(8,128)S(1)} collective-permute-done((f32[160,128]{1,0:T(8,128)S(1)}, f32[160,128]{1,0:T(8,128)S(1)}, u32[]{:S(2)}, u32[]{:S(2)}) %collective-permute-start.4) | collective-permute-done | bytes 81952 | tf_op jit(solution)/shard_map/ppermute | solution.py:152
  17.6 0.1 collective-permute-start.5
  17.7 1.3 %collective-permute-done.5 = f32[160,128]{1,0:T(8,128)S(1)} collective-permute-done((f32[160,128]{1,0:T(8,128)S(1)}, f32[160,128]{1,0:T(8,128)S(1)}, u32[]{:S(2)}, u32[]{:S(2)}) %collective-permute-start.5) | collective-permute-done | bytes 81952 | tf_op jit(solution)/shard_map/ppermute | solution.py:105
  19.0 0.1 fusion.4
  19.1 0.1 copy.11
  19.1 0.1 copy.8
  19.2 0.1 copy.9
  19.3 0.8 %maximum_multiply_fusion.g_ref = f32[256,256]{1,0:T(8,128)} fusion(f32[64,64]{1,0:T(8,128)S(1)} %get-tuple-element.12, f32[64,64]{1,0:T(8,128)S(1)} %copy.8, f32[64,128]{1,0:T(8,128)S(1)} %get-tuple-element.10, f32[128,128]{1,0:T(8,128)S(1)} %copy.9, f32[128,128]{1,0:T(8,128)S(1)} %get-tuple-element.15, f32[64,64]{1,0:T(8,128)S(1)} %get-tuple-element.14, ...), kind=kLoop, calls=%fused_computation | loop fusion | flops 524288 | bytes 524288 | tf_op jit(solution)/shard_map/div | solution.py:166
  20.1 15.8 %shard_map.28 = bf16[256,640]{1,0:T(8,128)(2,1)} custom-call(f32[256,256]{1,0:T(8,128)} %maximum_multiply_fusion.g_ref, bf16[640,256]{1,0:T(8,128)(2,1)} %cube_hbm.1, bf16[256,256]{1,0:T(8,128)(2,1)} %constant.38.clone.table_hbm), custom_call_target="tpu_custom_call" | custom-call | tf_op jit(solution)/shard_map/pallas_call | solution.py:53
  35.9 17.8 %all_to_all.5 = bf16[8,32,640]{2,1,0:T(8,128)(2,1)S(1)} all-to-all(bf16[8,32,640]{2,1,0:T(8,128)(2,1)} %bitcast.9), channel_id=1, replica_groups=mesh['groups'=2,'pix'=4,'sub'=2,'inner'=2] {'pix','sub'}, dimensions={0} | all-to-all | bytes 655360 | tf_op jit(solution)/shard_map/all_to_all | solution.py:170
  53.8 0.8 %copy.10 = bf16[32,8,640]{2,1,0:T(8,128)(2,1)} copy(bf16[32,8,640]{2,0,1:T(8,128)(2,1)S(1)} %bitcast.10) | data formatting | bytes 655360 | tf_op jit(solution)/shard_map/transpose | solution.py:171
  (7 shorter events, 0.1 us)
Async XLA Ops:
  1.6 1.4 %collective-permute-start = (f32[160,128]{1,0:T(8,128)S(1)}, f32[160,128]{1,0:T(8,128)S(1)}, u32[]{:S(2)}, u32[]{:S(2)}) collective-permute-start(f32[160,128]{1,0:T(8,128)S(1)} %fusion), channel_id=1, source_target_pairs={{0,1},{1,0},{2,3},{3,2},{4,5},{5,4},{6,7},{7,6},{8,9},{9,8},{10,11... | collective-permute-start | bytes 245768 | tf_op jit(solution)/shard_map/ppermute | solution.py:100
  3.1 7.0 %collective-permute-start.3 = (f32[160,128]{1,0:T(8,128)S(1)}, f32[160,128]{1,0:T(8,128)S(1)}, u32[]{:S(2)}, u32[]{:S(2)}) collective-permute-start(f32[160,128]{1,0:T(8,128)S(1)} %select_add_fusion), channel_id=1, source_target_pairs={{0,6},{2,4},{4,2},{6,0},{8,14},{10,12},{12,10},{14,8},{1,7},{3,5},... | collective-permute-start | bytes 245768 | tf_op jit(solution)/shard_map/ppermute | solution.py:138
  7.0 4.7 %collective-permute-start.2 = (f32[160,128]{1,0:T(8,128)S(1)}, f32[160,128]{1,0:T(8,128)S(1)}, u32[]{:S(2)}, u32[]{:S(2)}) collective-permute-start(f32[160,128]{1,0:T(8,128)S(1)} %select_add_fusion), channel_id=1, source_target_pairs={{0,4},{4,0},{8,12},{12,8},{1,5},{5,1},{9,13},{13,9},{2,6},{6,2},{1... | collective-permute-start | bytes 245768 | tf_op jit(solution)/shard_map/ppermute | solution.py:131
  7.4 4.4 %collective-permute-start.1 = (f32[160,128]{1,0:T(8,128)S(1)}, f32[160,128]{1,0:T(8,128)S(1)}, u32[]{:S(2)}, u32[]{:S(2)}) collective-permute-start(f32[160,128]{1,0:T(8,128)S(1)} %select_add_fusion), channel_id=1, source_target_pairs={{0,2},{2,0},{1,3},{3,1},{4,6},{6,4},{5,7},{7,5},{8,10},{10,8},{9,1... | collective-permute-start | bytes 245768 | tf_op jit(solution)/shard_map/ppermute | solution.py:130
  11.9 5.7 %collective-permute-start.4 = (f32[160,128]{1,0:T(8,128)S(1)}, f32[160,128]{1,0:T(8,128)S(1)}, u32[]{:S(2)}, u32[]{:S(2)}) collective-permute-start(f32[160,128]{1,0:T(8,128)S(1)} %add_add_fusion), channel_id=1, source_target_pairs={{0,8},{4,12},{8,0},{12,4},{1,9},{5,13},{9,1},{13,5},{2,10},{6,14},... | collective-permute-start | bytes 245768 | tf_op jit(solution)/shard_map/ppermute | solution.py:152
  17.6 1.3 %collective-permute-start.5 = (f32[160,128]{1,0:T(8,128)S(1)}, f32[160,128]{1,0:T(8,128)S(1)}, u32[]{:S(2)}, u32[]{:S(2)}) collective-permute-start(f32[160,128]{1,0:T(8,128)S(1)} %add.26), channel_id=1, source_target_pairs={{0,1},{1,0},{2,3},{3,2},{4,5},{5,4},{6,7},{7,6},{8,9},{9,8},{10,11... | collective-permute-start | bytes 245768 | tf_op jit(solution)/shard_map/ppermute | solution.py:105
